TPU v7x, 512 devices: a whole 4x8x8 slice. The times are simulated.
512 devices in a mesh: space: 64 (over z, x, core), snap: 8 (over y).
Axes of the slice: x: 4, y: 8, z: 8, core: 2. Of those that a mesh axis runs over, the one named last changes fastest.
Arguments:
- snapshots: bfloat16 [262144, 2048], P('space', 'snap'), may hold values from -6 to 6
- basis: bfloat16 [262144, 64], P('space'), may hold values from -0.01171875 to 0.01171875
Outputs:
- normal: float32 [2144, 2144], P('snap')
- rhs: float32 [2144, 64], P('snap')
All inputs are finite; a program needn't handle non-finite values.
Results may differ from a plain program's by a relative error of at most 0.0034.
Values sent between devices are 32-bit elements; how exact they have to be, the bound alone decides.
No kernel may reach another device: no remote copies, remote signals or barrier semaphores. Data moves between devices by JAX's collectives and lax.ppermute only.
A program may use at most 64 MiB of HBM per device.

v0:
```python
import jax
import jax.numpy as jnp
import numpy as np
from jax import lax
from jax.sharding import PartitionSpec as P


def shifted(block, axis, distance):
    devices = range(lax.axis_size(axis))
    route = [((i - distance) % len(devices), i) for i in devices]
    return lax.ppermute(block, axis, route)


def row_block(states, diffs, total_snaps):
    rank = states.shape[0]
    upper_rows, upper_cols = np.triu_indices(rank)
    quad = states[upper_rows, :] * states[upper_cols, :]
    features = jnp.concatenate([states, quad], axis=0).T.astype(jnp.bfloat16)
    targets = diffs.T.astype(jnp.bfloat16)
    width = features.shape[1]
    block_rows = width // lax.axis_size("snap")
    chosen = lax.dynamic_slice_in_dim(features, lax.axis_index("snap") * block_rows, block_rows, 1)
    dims = (((0,), (0,)), ((), ()))
    normal = (
        lax.dot_general(chosen, features, dims, preferred_element_type=jnp.float32) / total_snaps
    )
    rhs = lax.dot_general(chosen, targets, dims, preferred_element_type=jnp.float32) / total_snaps
    return (normal, rhs)


def per_device(snapshots, basis):
    partial_value = lax.dot_general(
        basis, snapshots, (((0,), (0,)), ((), ())), preferred_element_type=jnp.float32
    )
    total_snaps = snapshots.shape[1] * lax.axis_size("snap")
    following = shifted(partial_value[:, :1], "snap", -1)
    groups = lax.axis_size("space")
    rank, columns = partial_value.shape
    width = columns // groups
    blocks = partial_value.reshape(rank, groups, width)
    nexts = jnp.concatenate([partial_value[:, width::width], following], axis=1)
    extended = jnp.concatenate([blocks, nexts[:, :, None]], axis=2)
    share = lax.psum_scatter(extended, "space", scatter_dimension=1, tiled=True)
    gathered = lax.all_gather(share, "snap", axis=1, tiled=True)
    states = gathered[:, :, :width].reshape(rank, -1)
    diffs = (gathered[:, :, 1:] - gathered[:, :, :width]).reshape(rank, -1)
    normal_part, rhs_part = row_block(states, diffs, total_snaps)
    normal, rhs = lax.psum((normal_part, rhs_part), "space")
    return (normal, rhs)


def solution(mesh):
    return jax.shard_map(
        per_device,
        mesh=mesh,
        in_specs=(P("space", "snap"), P("space", None)),
        out_specs=(P("snap", None), P("snap", None)),
        check_vma=False,
    )
```

profile of v0, /device:TPU:1, one launch (start us, length us, event | category | flops | bytes accessed | tf_op | source)
XLA Modules:
  0.0 460.8 jit_solution(5173694295732796001)
XLA Ops:
  7.2 0.0 copy-start
  7.2 0.0 copy-start.3
  7.2 0.0 copy-start.2
  7.2 0.0 all-reduce.5.cloned.1.call-start
  7.2 1.5 copy-done
  8.8 1.5 fusion.6
  10.3 5.9 %collective-permute-start = (f32[64,1]{1,0:T(8,128)S(1)}, f32[64,1]{1,0:T(8,128)S(1)}, u32[]{:S(2)}, u32[]{:S(2)}) collective-permute-start(f32[64,1]{1,0:T(8,128)S(1)} %slice.21), channel_id=1, source_target_pairs={{1,0},{2,1},{3,2},{4,3},{5,4},{6,5},{7,6},{0,7},{9,8},{10,9},{11,1... | collective-permute-start | bytes 776 | tf_op jit(solution)/shard_map/ppermute | solution.py:11
  16.2 0.0 copy-done.3
  16.2 0.6 slice.13
  16.8 0.1 copy.19
  16.9 0.3 collective-permute-done
  17.2 0.1 maximum_bitcast_fusion
  17.3 0.1 copy.20
  17.4 0.8 pad_maximum_fusion
  18.1 0.0 all-reduce.5.cloned.1.call-update
  18.2 0.0 all-reduce.7.cloned.1.call-start
  18.2 0.0 copy-done.2
  18.2 1.3 dynamic-slice.4
  19.5 192.4 %all-reduce.5.cloned.1.call-done = f32[64,64,5]{0,2,1:T(8,128)} async-done(((f32[64,64,5]{0,2,1:T(8,128)}), f32[64,64,5]{0,2,1:T(8,128)}) %all-reduce.5.cloned.1.call-update) | async-done | bytes 81936
  211.9 1.3 constant_dynamic-slice_fusion
  213.2 19.3 %all_gather.3 = f32[64,8,5]{0,2,1:T(8,128)S(1)} all-gather(f32[64,1,5]{0,2,1:T(8,128)S(1)} %constant_dynamic-slice_fusion), channel_id=1, replica_groups=mesh['space'=64,'snap'=8] {'snap'}, dimensions={1}, use_global_device_ids=true | all-gather | bytes 11520 | tf_op jit(solution)/shard_map/all_gather | solution.py:44
  232.6 0.1 copy.21
  232.6 3.9 gather_fusion.1
  236.6 0.3 copy.24
  236.9 4.0 gather_fusion
  240.9 1.1 copy.23
  241.9 1.0 multiply_convert_fusion
  242.9 2.0 convolution_multiply_fusion
  245.0 0.9 convolution_multiply_fusion.1
  245.8 0.0 all-reduce.7.cloned.1.call-update
  245.9 204.2 %all-reduce.7.cloned.1.call-done = (f32[268,2144]{1,0:T(8,128)}, f32[268,64]{0,1:T(8,128)}) async-done(((f32[268,2144]{1,0:T(8,128)}, f32[268,64]{0,1:T(8,128)}), (f32[268,2144]{1,0:T(8,128)}, f32[268,64]{0,1:T(8,128)})) %all-reduce.7.cloned.1.call-update) | async-done | bytes 2366992 | tf_op jit(solution)/shard_map/psum | solution.py:48
  450.1 0.0 copy-start.1
  450.1 3.3 copy.28
  453.3 0.0 copy-done.1
  453.3 0.6 copy.29
  (5 shorter events, 0.0 us)
Async XLA Ops:
  7.2 1.6 copy-start
  7.2 9.0 %copy-start.3 = (s32[2080]{0:T(1024)S(1)}, s32[2080]{0:T(1024)}, u32[]{:S(2)}) copy-start(s32[2080]{0:T(1024)} %constant.28) | copy-start | bytes 24964
  7.2 11.0 %copy-start.2 = (s32[2080]{0:T(1024)S(1)}, s32[2080]{0:T(1024)}, u32[]{:S(2)}) copy-start(s32[2080]{0:T(1024)} %constant.29) | copy-start | bytes 24964
  7.2 204.7 %all-reduce.5.cloned.1.call-start = ((), (), s32[]{:S(2)}) async-start(), calls=%async_computation | async-start | bytes 524288
  10.3 6.9 %collective-permute-start = (f32[64,1]{1,0:T(8,128)S(1)}, f32[64,1]{1,0:T(8,128)S(1)}, u32[]{:S(2)}, u32[]{:S(2)}) collective-permute-start(f32[64,1]{1,0:T(8,128)S(1)} %slice.21), channel_id=1, source_target_pairs={{1,0},{2,1},{3,2},{4,3},{5,4},{6,5},{7,6},{0,7},{9,8},{10,9},{11,1... | collective-permute-start | bytes 776 | tf_op jit(solution)/shard_map/ppermute | solution.py:11
  18.2 431.9 %all-reduce.7.cloned.1.call-start = ((), (), s32[]{:S(2)}) async-start(), calls=%async_computation.1 | async-start | bytes 4931584 | tf_op jit(solution)/shard_map/psum | solution.py:48
  450.1 3.3 copy-start.1
Sparse Core Ops, SparseCore 0:
  18.3 193.5 all-reduce.4
  246.0 204.0 all-reduce.6
where the time goes:
time: 462 us; the launch traced here: 461 us
  waiting for transfers between devices  397 us (86%)
  blocking collectives  19.3 us (4%)
  local copies, waits for them, and re-layouts  18.2 us (4%)
  between operations  14.2 us (3%)
  starting transfers between devices  5.99 us (1%)
    psum x1, waiting for transfers between devices, per_device(): normal, rhs = lax.psum((normal_part, rhs_part), 'space')  204 us
    unnamed x3, waiting for transfers between devices  192 us
    all_gather x1, blocking collectives, per_device(): gathered = lax.all_gather(share, 'snap', axis=1, tiled=True)  19.3 us
    gather x4, local copies, waits for them, and re-layouts, row_block(): quad = states[upper_rows, :] * states[upper_cols, :]  9.28 us
  transfers between devices with their start and end apart: 3, of which 3 were waited for; matrix products, arithmetic and copies ran while one was open for 0% of the time, Pallas kernels for 0%

commit v1 on v0

v1 whole, which is shorter than its diff:
```python
import jax
import jax.numpy as jnp
import numpy as np
from jax import lax
from jax.experimental import pallas as pl
from jax.experimental.pallas import tpu as pltpu
from jax.sharding import PartitionSpec as P


def swapped(block, axis, distance):
    count = lax.axis_size(axis)
    return lax.ppermute(block, axis, [(i, i ^ distance) for i in range(count)])


def butterfly_sum(block, axis):
    distance = 1
    while distance < lax.axis_size(axis):
        block = block + swapped(block, axis, distance)
        distance *= 2
    return block


def butterfly_gather(block, axis):
    index = lax.axis_index(axis)
    distance = 1
    while distance < lax.axis_size(axis):
        other = swapped(block, axis, distance)
        low = (index // distance) % 2 == 0
        block = jnp.where(
            low,
            jnp.concatenate([block, other], axis=1),
            jnp.concatenate([other, block], axis=1),
        )
        distance *= 2
    return block


def feature_kernel(states_ref, out_ref, rows_ref):
    rank = states_ref.shape[0]
    rows_ref[0:rank, :] = states_ref[...]
    offset = rank
    for a in range(rank):
        count = rank - a
        rows_ref[offset : offset + count, :] = states_ref[a : a + 1, :] * states_ref[a:rank, :]
        offset += count
    out_ref[...] = rows_ref[...].astype(out_ref.dtype)


def features_t(states, lanes=256):
    rank, snaps = states.shape
    width = rank + rank * (rank + 1) // 2
    return pl.pallas_call(
        feature_kernel,
        grid=(snaps // lanes,),
        in_specs=[pl.BlockSpec((rank, lanes), lambda j: (0, j))],
        out_specs=pl.BlockSpec((width, lanes), lambda j: (0, j)),
        out_shape=jax.ShapeDtypeStruct((width, snaps), jnp.bfloat16),
        scratch_shapes=[pltpu.VMEM((width, lanes), jnp.float32)],
        cost_estimate=pl.CostEstimate(
            flops=width * snaps, transcendentals=0, bytes_accessed=rank * snaps * 4 + width * snaps * 2
        ),
    )(states)


def per_device(snapshots, basis):
    partial_value = lax.dot_general(
        basis, snapshots, (((0,), (0,)), ((), ())), preferred_element_type=jnp.float32
    )
    reduced = butterfly_sum(partial_value, "space")
    states = butterfly_gather(reduced, "snap")
    total_snaps = states.shape[1]
    feats = features_t(states)
    targets = (jnp.roll(states, -1, axis=1) - states).astype(jnp.bfloat16)
    width = feats.shape[0]
    block_rows = width // lax.axis_size("snap")
    chosen = lax.dynamic_slice_in_dim(feats, lax.axis_index("snap") * block_rows, block_rows, 0)
    dims = (((1,), (1,)), ((), ()))
    normal = lax.dot_general(chosen, feats, dims, preferred_element_type=jnp.float32) / total_snaps
    rhs = lax.dot_general(chosen, targets, dims, preferred_element_type=jnp.float32) / total_snaps
    return (normal, rhs)


def solution(mesh):
    return jax.shard_map(
        per_device,
        mesh=mesh,
        in_specs=(P("space", "snap"), P("space", None)),
        out_specs=(P("snap", None), P("snap", None)),
        check_vma=False,
    )
```

time: 462 us -> 104 us (0.23)
  the two profiles are of different devices: /device:TPU:1 before, /device:TPU:2 now
where the time goes in v1:
time: 104 us; the launch traced here: 103 us
  starting transfers between devices  42.6 us (41%)
  waiting for transfers between devices  37.5 us (36%)
  matrix products  12 us (12%)
  Pallas kernels  7.36 us (7%)
  local copies, waits for them, and re-layouts  2.42 us (2%)
    ppermute x9, starting transfers between devices, swapped(): return lax.ppermute(block, axis, [(i, i ^ distance) for i in range(count)])  42.6 us
    ppermute x9, waiting for transfers between devices, swapped(): return lax.ppermute(block, axis, [(i, i ^ distance) for i in range(count)])  37.5 us
    dot_general x1, matrix products, per_device(): lax.dot_general(chosen, feats, dims, preferred_element_type=jnp.float32)  8.12 us
    pallas_call x1, Pallas kernels, features_t(): pl.pallas_call(feature_kernel, grid=(snaps // lanes,), in_specs=[pl.Block...  7.36 us
    dot_general x1, matrix products, per_device(): lax.dot_general(chosen, targets, dims, preferred_element_type=jnp.float32)  2.41 us
    unnamed x6, local copies, waits for them, and re-layouts  2.22 us
  transfers between devices with their start and end apart: 9, of which 9 were waited for; matrix products, arithmetic and copies ran while one was open for 0% of the time, Pallas kernels for 0%

profile of v1, /device:TPU:2, one launch (start us, length us, event | category | flops | bytes accessed | tf_op | source)
XLA Modules:
  0.0 102.8 jit_solution(3312723223204240340)
XLA Ops:
  0.6 0.0 copy-start
  0.6 1.6 %copy-done = bf16[4096,256]{1,0:T(8,128)(2,1)S(1)} copy-done((bf16[4096,256]{1,0:T(8,128)(2,1)S(1)}, bf16[4096,256]{1,0:T(8,128)(2,1)}, u32[]{:S(2)}) %copy-start) | copy-done | bytes 2097176
  2.2 1.5 %fusion.7 = f32[64,256]{1,0:T(8,128)S(1)} fusion(bf16[4096,64]{0,1:T(8,128)(2,1)} %param.3, bf16[4096,256]{1,0:T(8,128)(2,1)S(1)} %copy-done), kind=kOutput, calls=%fused_computation.12 | convolution fusion | flops 134217728 | bytes 2686976 | tf_op jit(solution)/shard_map/dot_general | solution.py:66
  3.7 1.9 %collective-permute-start = (f32[64,256]{1,0:T(8,128)S(1)}, f32[64,256]{1,0:T(8,128)S(1)}, u32[]{:S(2)}, u32[]{:S(2)}) collective-permute-start(f32[64,256]{1,0:T(8,128)S(1)} %fusion.7), channel_id=1, source_target_pairs={{0,8},{8,0},{16,24},{24,16},{32,40},{40,32},{48,56},{56,48},{64,72... | collective-permute-start | bytes 196616 | tf_op jit(solution)/shard_map/ppermute | solution.py:12
  5.7 1.2 %collective-permute-done = f32[64,256]{1,0:T(8,128)S(1)} collective-permute-done((f32[64,256]{1,0:T(8,128)S(1)}, f32[64,256]{1,0:T(8,128)S(1)}, u32[]{:S(2)}, u32[]{:S(2)}) %collective-permute-start) | collective-permute-done | bytes 65568 | tf_op jit(solution)/shard_map/ppermute | solution.py:12
  6.9 7.8 %collective-permute-start.1 = (f32[64,256]{1,0:T(8,128)S(1)}, f32[64,256]{1,0:T(8,128)S(1)}, u32[]{:S(2)}, u32[]{:S(2)}) collective-permute-start(f32[64,256]{1,0:T(8,128)S(1)} %add.37), channel_id=1, source_target_pairs={{0,16},{8,24},{16,0},{24,8},{32,48},{40,56},{48,32},{56,40},{64,80... | collective-permute-start | bytes 196616 | tf_op jit(solution)/shard_map/ppermute | solution.py:12
  14.7 2.4 %collective-permute-done.1 = f32[64,256]{1,0:T(8,128)S(1)} collective-permute-done((f32[64,256]{1,0:T(8,128)S(1)}, f32[64,256]{1,0:T(8,128)S(1)}, u32[]{:S(2)}, u32[]{:S(2)}) %collective-permute-start.1) | collective-permute-done | bytes 65568 | tf_op jit(solution)/shard_map/ppermute | solution.py:12
  17.1 1.9 %collective-permute-start.2 = (f32[64,256]{1,0:T(8,128)S(1)}, f32[64,256]{1,0:T(8,128)S(1)}, u32[]{:S(2)}, u32[]{:S(2)}) collective-permute-start(f32[64,256]{1,0:T(8,128)S(1)} %add.38), channel_id=1, source_target_pairs={{0,32},{8,40},{16,48},{24,56},{32,0},{40,8},{48,16},{56,24},{64,96... | collective-permute-start | bytes 196616 | tf_op jit(solution)/shard_map/ppermute | solution.py:12
  19.0 5.7 %collective-permute-done.2 = f32[64,256]{1,0:T(8,128)S(1)} collective-permute-done((f32[64,256]{1,0:T(8,128)S(1)}, f32[64,256]{1,0:T(8,128)S(1)}, u32[]{:S(2)}, u32[]{:S(2)}) %collective-permute-start.2) | collective-permute-done | bytes 65568 | tf_op jit(solution)/shard_map/ppermute | solution.py:12
  24.8 1.9 %collective-permute-start.3 = (f32[64,256]{1,0:T(8,128)S(1)}, f32[64,256]{1,0:T(8,128)S(1)}, u32[]{:S(2)}, u32[]{:S(2)}) collective-permute-start(f32[64,256]{1,0:T(8,128)S(1)} %add.39), channel_id=1, source_target_pairs={{0,64},{8,72},{16,80},{24,88},{32,96},{40,104},{48,112},{56,120},{... | collective-permute-start | bytes 196616 | tf_op jit(solution)/shard_map/ppermute | solution.py:12
  26.7 4.2 %collective-permute-done.3 = f32[64,256]{1,0:T(8,128)S(1)} collective-permute-done((f32[64,256]{1,0:T(8,128)S(1)}, f32[64,256]{1,0:T(8,128)S(1)}, u32[]{:S(2)}, u32[]{:S(2)}) %collective-permute-start.3) | collective-permute-done | bytes 65568 | tf_op jit(solution)/shard_map/ppermute | solution.py:12
  31.0 2.4 %collective-permute-start.4 = (f32[64,256]{1,0:T(8,128)S(1)}, f32[64,256]{1,0:T(8,128)S(1)}, u32[]{:S(2)}, u32[]{:S(2)}) collective-permute-start(f32[64,256]{1,0:T(8,128)S(1)} %add.40), channel_id=1, source_target_pairs={{0,128},{8,136},{16,144},{24,152},{32,160},{40,168},{48,176},{56,1... | collective-permute-start | bytes 196616 | tf_op jit(solution)/shard_map/ppermute | solution.py:12
  33.4 4.8 %collective-permute-done.4 = f32[64,256]{1,0:T(8,128)S(1)} collective-permute-done((f32[64,256]{1,0:T(8,128)S(1)}, f32[64,256]{1,0:T(8,128)S(1)}, u32[]{:S(2)}, u32[]{:S(2)}) %collective-permute-start.4) | collective-permute-done | bytes 65568 | tf_op jit(solution)/shard_map/ppermute | solution.py:12
  38.2 6.7 %collective-permute-start.5 = (f32[64,256]{1,0:T(8,128)S(1)}, f32[64,256]{1,0:T(8,128)S(1)}, u32[]{:S(2)}, u32[]{:S(2)}) collective-permute-start(f32[64,256]{1,0:T(8,128)S(1)} %add.41), channel_id=1, source_target_pairs={{0,256},{8,264},{16,272},{24,280},{32,288},{40,296},{48,304},{56,3... | collective-permute-start | bytes 196616 | tf_op jit(solution)/shard_map/ppermute | solution.py:12
  44.9 3.5 %collective-permute-done.5 = f32[64,256]{1,0:T(8,128)S(1)} collective-permute-done((f32[64,256]{1,0:T(8,128)S(1)}, f32[64,256]{1,0:T(8,128)S(1)}, u32[]{:S(2)}, u32[]{:S(2)}) %collective-permute-start.5) | collective-permute-done | bytes 65568 | tf_op jit(solution)/shard_map/ppermute | solution.py:12
  48.4 2.9 %collective-permute-start.6 = (f32[64,256]{1,0:T(8,128)S(1)}, f32[64,256]{1,0:T(8,128)S(1)}, u32[]{:S(2)}, u32[]{:S(2)}) collective-permute-start(f32[64,256]{1,0:T(8,128)S(1)} %add.42), channel_id=1, source_target_pairs={{0,1},{1,0},{2,3},{3,2},{4,5},{5,4},{6,7},{7,6},{8,9},{9,8},{10,11... | collective-permute-start | bytes 196616 | tf_op jit(solution)/shard_map/ppermute | solution.py:12
  51.4 3.3 %collective-permute-done.6 = f32[64,256]{1,0:T(8,128)S(1)} collective-permute-done((f32[64,256]{1,0:T(8,128)S(1)}, f32[64,256]{1,0:T(8,128)S(1)}, u32[]{:S(2)}, u32[]{:S(2)}) %collective-permute-start.6) | collective-permute-done | bytes 65568 | tf_op jit(solution)/shard_map/ppermute | solution.py:12
  54.7 4.0 %collective-permute-start.7 = (f32[64,512]{1,0:T(8,128)S(1)}, f32[64,512]{1,0:T(8,128)S(1)}, u32[]{:S(2)}, u32[]{:S(2)}) collective-permute-start(f32[64,512]{1,0:T(8,128)S(1)} %maximum_select_fusion.2), channel_id=1, source_target_pairs={{0,2},{1,3},{2,0},{3,1},{4,6},{5,7},{6,4},{7,5},{8,10},{9,11},{10,... | collective-permute-start | bytes 393224 | tf_op jit(solution)/shard_map/ppermute | solution.py:12
  58.7 5.2 %collective-permute-done.7 = f32[64,512]{1,0:T(8,128)S(1)} collective-permute-done((f32[64,512]{1,0:T(8,128)S(1)}, f32[64,512]{1,0:T(8,128)S(1)}, u32[]{:S(2)}, u32[]{:S(2)}) %collective-permute-start.7) | collective-permute-done | bytes 131104 | tf_op jit(solution)/shard_map/ppermute | solution.py:12
  63.9 13.0 %collective-permute-start.8 = (f32[64,1024]{1,0:T(8,128)S(1)}, f32[64,1024]{1,0:T(8,128)S(1)}, u32[]{:S(2)}, u32[]{:S(2)}) collective-permute-start(f32[64,1024]{1,0:T(8,128)S(1)} %maximum_select_fusion.1), channel_id=1, source_target_pairs={{0,4},{1,5},{2,6},{3,7},{4,0},{5,1},{6,2},{7,3},{8,12},{9,13},{10,... | collective-permute-start | bytes 786440 | tf_op jit(solution)/shard_map/ppermute | solution.py:12
  76.9 7.1 %collective-permute-done.8 = f32[64,1024]{1,0:T(8,128)S(1)} collective-permute-done((f32[64,1024]{1,0:T(8,128)S(1)}, f32[64,1024]{1,0:T(8,128)S(1)}, u32[]{:S(2)}, u32[]{:S(2)}) %collective-permute-start.8) | collective-permute-done | bytes 262176 | tf_op jit(solution)/shard_map/ppermute | solution.py:12
  84.1 0.0 copy-start.1
  84.1 0.2 slice.10
  84.3 0.6 copy-done.1
  84.9 7.4 %shard_map.41 = bf16[2144,2048]{1,0:T(8,128)(2,1)} custom-call(f32[64,2048]{1,0:T(8,128)} %copy-done.1), custom_call_target="tpu_custom_call" | custom-call | flops 4390912 | bytes 9306112 | tf_op jit(solution)/shard_map/pallas_call | solution.py:52
  92.3 0.0 copy-start.2
  92.3 0.0 slice-start
  92.3 8.1 %convolution_multiply_fusion = f32[268,2144]{1,0:T(8,128)} fusion(bf16[2144,2048]{1,0:T(8,128)(2,1)} %shard_map.41, s32[]{:T(128)S(6)} %select_n.61), kind=kOutput, calls=%fused_computation | convolution fusion | flops 2354103296 | bytes 12194308 | tf_op jit(solution)/shard_map/dot_general | solution.py:78
  100.4 0.0 copy-done.2
  100.4 0.0 slice-done
  100.4 2.4 %convolution_multiply_fusion.1 = f32[268,64]{0,1:T(8,128)} fusion(bf16[2144,2048]{1,0:T(8,128)(2,1)} %shard_map.41, s32[]{:T(128)S(6)} %select_n.61, f32[64,2048]{1,0:T(8,128)S(1)} %copy-done.2, f32[64,1]{1,0:T(8,128)S(1)} %slice-done, f32[64,2047]{1,0:T(8,128)S(1)} %slice.10), kind=kOutput, calls=%fused_computation.1 | convolution fusion | flops 70664960 | bytes 2231300 | tf_op jit(solution)/shard_map/dot_general | solution.py:79
  (9 shorter events, 0.1 us)
Async XLA Ops:
  0.6 1.6 %copy-start = (bf16[4096,256]{1,0:T(8,128)(2,1)S(1)}, bf16[4096,256]{1,0:T(8,128)(2,1)}, u32[]{:S(2)}) copy-start(bf16[4096,256]{1,0:T(8,128)(2,1)} %param.2) | copy-start | bytes 6291460
  3.7 3.1 %collective-permute-start = (f32[64,256]{1,0:T(8,128)S(1)}, f32[64,256]{1,0:T(8,128)S(1)}, u32[]{:S(2)}, u32[]{:S(2)}) collective-permute-start(f32[64,256]{1,0:T(8,128)S(1)} %fusion.7), channel_id=1, source_target_pairs={{0,8},{8,0},{16,24},{24,16},{32,40},{40,32},{48,56},{56,48},{64,72... | collective-permute-start | bytes 196616 | tf_op jit(solution)/shard_map/ppermute | solution.py:12
  6.9 10.2 %collective-permute-start.1 = (f32[64,256]{1,0:T(8,128)S(1)}, f32[64,256]{1,0:T(8,128)S(1)}, u32[]{:S(2)}, u32[]{:S(2)}) collective-permute-start(f32[64,256]{1,0:T(8,128)S(1)} %add.37), channel_id=1, source_target_pairs={{0,16},{8,24},{16,0},{24,8},{32,48},{40,56},{48,32},{56,40},{64,80... | collective-permute-start | bytes 196616 | tf_op jit(solution)/shard_map/ppermute | solution.py:12
  17.1 7.7 %collective-permute-start.2 = (f32[64,256]{1,0:T(8,128)S(1)}, f32[64,256]{1,0:T(8,128)S(1)}, u32[]{:S(2)}, u32[]{:S(2)}) collective-permute-start(f32[64,256]{1,0:T(8,128)S(1)} %add.38), channel_id=1, source_target_pairs={{0,32},{8,40},{16,48},{24,56},{32,0},{40,8},{48,16},{56,24},{64,96... | collective-permute-start | bytes 196616 | tf_op jit(solution)/shard_map/ppermute | solution.py:12
  24.8 6.2 %collective-permute-start.3 = (f32[64,256]{1,0:T(8,128)S(1)}, f32[64,256]{1,0:T(8,128)S(1)}, u32[]{:S(2)}, u32[]{:S(2)}) collective-permute-start(f32[64,256]{1,0:T(8,128)S(1)} %add.39), channel_id=1, source_target_pairs={{0,64},{8,72},{16,80},{24,88},{32,96},{40,104},{48,112},{56,120},{... | collective-permute-start | bytes 196616 | tf_op jit(solution)/shard_map/ppermute | solution.py:12
  31.0 7.2 %collective-permute-start.4 = (f32[64,256]{1,0:T(8,128)S(1)}, f32[64,256]{1,0:T(8,128)S(1)}, u32[]{:S(2)}, u32[]{:S(2)}) collective-permute-start(f32[64,256]{1,0:T(8,128)S(1)} %add.40), channel_id=1, source_target_pairs={{0,128},{8,136},{16,144},{24,152},{32,160},{40,168},{48,176},{56,1... | collective-permute-start | bytes 196616 | tf_op jit(solution)/shard_map/ppermute | solution.py:12
  38.2 10.2 %collective-permute-start.5 = (f32[64,256]{1,0:T(8,128)S(1)}, f32[64,256]{1,0:T(8,128)S(1)}, u32[]{:S(2)}, u32[]{:S(2)}) collective-permute-start(f32[64,256]{1,0:T(8,128)S(1)} %add.41), channel_id=1, source_target_pairs={{0,256},{8,264},{16,272},{24,280},{32,288},{40,296},{48,304},{56,3... | collective-permute-start | bytes 196616 | tf_op jit(solution)/shard_map/ppermute | solution.py:12
  48.4 6.3 %collective-permute-start.6 = (f32[64,256]{1,0:T(8,128)S(1)}, f32[64,256]{1,0:T(8,128)S(1)}, u32[]{:S(2)}, u32[]{:S(2)}) collective-permute-start(f32[64,256]{1,0:T(8,128)S(1)} %add.42), channel_id=1, source_target_pairs={{0,1},{1,0},{2,3},{3,2},{4,5},{5,4},{6,7},{7,6},{8,9},{9,8},{10,11... | collective-permute-start | bytes 196616 | tf_op jit(solution)/shard_map/ppermute | solution.py:12
  54.7 9.2 %collective-permute-start.7 = (f32[64,512]{1,0:T(8,128)S(1)}, f32[64,512]{1,0:T(8,128)S(1)}, u32[]{:S(2)}, u32[]{:S(2)}) collective-permute-start(f32[64,512]{1,0:T(8,128)S(1)} %maximum_select_fusion.2), channel_id=1, source_target_pairs={{0,2},{1,3},{2,0},{3,1},{4,6},{5,7},{6,4},{7,5},{8,10},{9,11},{10,... | collective-permute-start | bytes 393224 | tf_op jit(solution)/shard_map/ppermute | solution.py:12
  63.9 20.1 %collective-permute-start.8 = (f32[64,1024]{1,0:T(8,128)S(1)}, f32[64,1024]{1,0:T(8,128)S(1)}, u32[]{:S(2)}, u32[]{:S(2)}) collective-permute-start(f32[64,1024]{1,0:T(8,128)S(1)} %maximum_select_fusion.1), channel_id=1, source_target_pairs={{0,4},{1,5},{2,6},{3,7},{4,0},{5,1},{6,2},{7,3},{8,12},{9,13},{10,... | collective-permute-start | bytes 786440 | tf_op jit(solution)/shard_map/ppermute | solution.py:12
  84.1 0.8 copy-start.1
  92.3 8.1 %copy-start.2 = (f32[64,2048]{1,0:T(8,128)S(1)}, f32[64,2048]{1,0:T(8,128)}, u32[]{:S(2)}) copy-start(f32[64,2048]{1,0:T(8,128)} %copy-done.1) | copy-start | bytes 1572868
  92.3 8.1 %slice-start = ((f32[64,2048]{1,0:T(8,128)}), f32[64,1]{1,0:T(8,128)S(1)}, s32[]{:S(2)}) async-start(f32[64,2048]{1,0:T(8,128)} %copy-done.1), calls=%async_computation | async-start | bytes 65536 | tf_op jit(solution)/shard_map/jit(_roll_static)/slice | solution.py:73

commit v2 on v1

--- a/solution.py
+++ b/solution.py
@@ -66,13 +66,22 @@
     partial_value = lax.dot_general(
         basis, snapshots, (((0,), (0,)), ((), ())), preferred_element_type=jnp.float32
     )
-    reduced = butterfly_sum(partial_value, "space")
-    states = butterfly_gather(reduced, "snap")
+    rank, columns = partial_value.shape
+    groups = lax.axis_size("space")
+    snaps = lax.axis_size("snap")
+    chunks = partial_value.reshape(rank, groups, columns // groups)
+    received = lax.all_to_all(chunks, "space", 1, 1, tiled=True)
+    owned = jnp.sum(received, axis=1)
+    spread = jnp.broadcast_to(owned[:, None, :], (rank, groups * snaps, owned.shape[1]))
+    everyone = lax.all_to_all(spread, ("space", "snap"), 1, 1, tiled=True)
+    states = (
+        everyone.reshape(rank, groups, snaps, -1).transpose(0, 2, 1, 3).reshape(rank, columns * snaps)
+    )
     total_snaps = states.shape[1]
     feats = features_t(states)
     targets = (jnp.roll(states, -1, axis=1) - states).astype(jnp.bfloat16)
     width = feats.shape[0]
-    block_rows = width // lax.axis_size("snap")
+    block_rows = width // snaps
     chosen = lax.dynamic_slice_in_dim(feats, lax.axis_index("snap") * block_rows, block_rows, 0)
     dims = (((1,), (1,)), ((), ()))
     normal = lax.dot_general(chosen, feats, dims, preferred_element_type=jnp.float32) / total_snaps

time: 104 us -> 92 us (0.88)
  the two profiles are of different devices: /device:TPU:2 before, /device:TPU:1 now
where the time goes in v2:
time: 92 us; the launch traced here: 91.3 us
  blocking collectives  24.7 us (27%)
  waiting for transfers between devices  22.7 us (25%)
  matrix products  12.5 us (14%)
  starting transfers between devices  10.9 us (12%)
  local copies, waits for them, and re-layouts  8.72 us (9%)
  Pallas kernels  7.38 us (8%)
  other arithmetic  3.66 us (4%)
    all_to_all x1, blocking collectives, per_device(): received = lax.all_to_all(chunks, 'space', 1, 1, tiled=True)  24.7 us
    all_to_all x1, waiting for transfers between devices, per_device(): everyone = lax.all_to_all(spread, ('space', 'snap'), 1, 1, tiled=True)  22.7 us
    all_to_all x1, starting transfers between devices, per_device(): everyone = lax.all_to_all(spread, ('space', 'snap'), 1, 1, tiled=True)  10.9 us
    dot_general x1, matrix products, per_device(): lax.dot_general(chosen, feats, dims, preferred_element_type=jnp.float32)  8.14 us
    pallas_call x1, Pallas kernels, features_t(): pl.pallas_call(feature_kernel, grid=(snaps // lanes,), in_specs=[pl.Block...  7.38 us
    unnamed x9, local copies, waits for them, and re-layouts  5.23 us
    all_to_all x1, other arithmetic, per_device(): everyone = lax.all_to_all(spread, ('space', 'snap'), 1, 1, tiled=True)  2.78 us
    dot_general x1, matrix products, per_device(): lax.dot_general(chosen, targets, dims, preferred_element_type=jnp.float32)  2.43 us
  transfers between devices with their start and end apart: 1, of which 1 were waited for; matrix products, arithmetic and copies ran while one was open for 0% of the time, Pallas kernels for 0%

profile of v2, /device:TPU:1, one launch (start us, length us, event | category | flops | bytes accessed | tf_op | source)
XLA Modules:
  0.0 91.3 jit_solution(9538212375653646249)
XLA Ops:
  0.6 0.0 copy-start
  0.6 1.6 %copy-done = bf16[4096,256]{1,0:T(8,128)(2,1)S(1)} copy-done((bf16[4096,256]{1,0:T(8,128)(2,1)S(1)}, bf16[4096,256]{1,0:T(8,128)(2,1)}, u32[]{:S(2)}) %copy-start) | copy-done | bytes 2097176
  2.2 2.0 %fusion.7 = f32[64,256]{0,1:T(8,128)S(1)} fusion(bf16[4096,64]{0,1:T(8,128)(2,1)} %param.3, bf16[4096,256]{1,0:T(8,128)(2,1)S(1)} %copy-done), kind=kOutput, calls=%fused_computation.12 | convolution fusion | flops 134217728 | bytes 2686976 | tf_op jit(solution)/shard_map/dot_general | solution.py:66
  4.2 0.1 reshape.17
  4.3 24.7 %all_to_all.10 = f32[64,1,256]{2,1,0:T(1,128)S(1)} all-to-all(f32[64,1,256]{2,1,0:T(1,128)S(1)} %reshape.17), channel_id=1, replica_groups=mesh['space'=64,'snap'=8] {'space'}, dimensions={0} | all-to-all | bytes 131072 | tf_op jit(solution)/shard_map/all_to_all | solution.py:73
  29.1 0.5 broadcast.3
  29.6 0.8 reduce
  30.4 0.1 reshape.18
  30.5 0.1 bitcast_reduce_fusion
  30.6 0.1 broadcast_bitcast_fusion
  30.7 1.8 %reshape.19 = f32[512,1,256]{2,1,0:T(1,128)} reshape(f32[512,4,64]{2,1,0:T(4,128)S(1)} %broadcast_bitcast_fusion) | data formatting | bytes 1048576
  32.5 10.9 %all-to-all-start.1 = ((f32[512,1,256]{2,1,0:T(1,128)}), f32[512,1,256]{2,1,0:T(1,128)S(1)}, u32[]{:S(2)}, u32[]{:S(2)}) async-start(f32[512,1,256]{2,1,0:T(1,128)} %reshape.19), calls=%async_computation.1 | async-start | bytes 1048576 | tf_op jit(solution)/shard_map/all_to_all | solution.py:76
  43.4 22.7 %all-to-all-done.1 = f32[512,1,256]{2,1,0:T(1,128)S(1)} async-done(((f32[512,1,256]{2,1,0:T(1,128)}), f32[512,1,256]{2,1,0:T(1,128)S(1)}, u32[]{:S(2)}, u32[]{:S(2)}) %all-to-all-start.1) | async-done | bytes 524320 | tf_op jit(solution)/shard_map/all_to_all | solution.py:76
  66.1 2.8 %reduce.1 = f32[512,256]{1,0:T(8,128)} reduce(f32[512,1,256]{2,1,0:T(1,128)S(1)} %all-to-all-done.1, f32[]{:T(128)} %broadcast.3), dimensions={1}, to_apply=%all_to_all.7.reduce_sub_computation | reduce | bytes 1048580 | tf_op jit(solution)/shard_map/all_to_all | solution.py:76
  68.9 1.5 %reshape.20 = f32[512,4,64]{2,1,0:T(4,128)S(1)} reshape(f32[512,256]{1,0:T(8,128)} %reduce.1) | data formatting | bytes 1048576
  70.4 0.1 copy.13
  70.5 0.7 copy.9
  71.1 1.1 %copy.10.states_ref = f32[64,2048]{1,0:T(8,128)} copy(f32[64,2048]{0,1:T(8,128)S(1)} %bitcast.16) | data formatting | bytes 1048576 | tf_op jit(solution)/shard_map/reshape | solution.py:78
  72.2 1.1 %slice.10 = f32[64,2047]{0,1:T(8,128)} slice(f32[64,2048]{0,1:T(8,128)S(1)} %bitcast.17), slice={[0:64], [1:2048]} | slice | bytes 1048064 | tf_op jit(solution)/shard_map/jit(_roll_static)/slice | solution.py:82
  73.4 7.4 %shard_map.41 = bf16[2144,2048]{1,0:T(8,128)(2,1)} custom-call(f32[64,2048]{1,0:T(8,128)} %copy.10.states_ref), custom_call_target="tpu_custom_call" | custom-call | flops 4390912 | bytes 9306112 | tf_op jit(solution)/shard_map/pallas_call | solution.py:52
  80.8 0.0 copy-start.1
  80.8 8.1 %convolution_multiply_fusion = f32[268,2144]{1,0:T(8,128)} fusion(bf16[2144,2048]{1,0:T(8,128)(2,1)} %shard_map.41, s32[]{:T(128)S(6)} %select_n.3), kind=kOutput, calls=%fused_computation | convolution fusion | flops 2354103296 | bytes 12194308 | tf_op jit(solution)/shard_map/dot_general | solution.py:87
  88.9 0.0 copy-done.1
  88.9 2.4 %convolution_multiply_fusion.1 = f32[268,64]{0,1:T(8,128)} fusion(bf16[2144,2048]{1,0:T(8,128)(2,1)} %shard_map.41, s32[]{:T(128)S(6)} %select_n.3, f32[64,2048]{0,1:T(8,128)S(1)} %bitcast.19, f32[64,1]{0,1:T(1,128)S(1)} %slice.11, f32[64,2047]{0,1:T(8,128)S(1)} %copy-done.1), kind=kOutput, calls=%fused_computation.1 | convolution fusion | flops 70664960 | bytes 2231300 | tf_op jit(solution)/shard_map/dot_general | solution.py:88
  (1 shorter events, 0.0 us)
Async XLA Ops:
  0.6 1.6 %copy-start = (bf16[4096,256]{1,0:T(8,128)(2,1)S(1)}, bf16[4096,256]{1,0:T(8,128)(2,1)}, u32[]{:S(2)}) copy-start(bf16[4096,256]{1,0:T(8,128)(2,1)} %param.2) | copy-start | bytes 6291460
  32.5 33.6 %all-to-all-start.1 = ((f32[512,1,256]{2,1,0:T(1,128)}), f32[512,1,256]{2,1,0:T(1,128)S(1)}, u32[]{:S(2)}, u32[]{:S(2)}) async-start(f32[512,1,256]{2,1,0:T(1,128)} %reshape.19), calls=%async_computation.1 | async-start | bytes 1048576 | tf_op jit(solution)/shard_map/all_to_all | solution.py:76
  80.8 8.1 %copy-start.1 = (f32[64,2047]{0,1:T(8,128)S(1)}, f32[64,2047]{0,1:T(8,128)}, u32[]{:S(2)}) copy-start(f32[64,2047]{0,1:T(8,128)} %slice.10) | copy-start | bytes 1572100

commit v3 on v1

--- a/solution.py
+++ b/solution.py
@@ -66,13 +66,19 @@
     partial_value = lax.dot_general(
         basis, snapshots, (((0,), (0,)), ((), ())), preferred_element_type=jnp.float32
     )
-    reduced = butterfly_sum(partial_value, "space")
-    states = butterfly_gather(reduced, "snap")
+    rank, columns = partial_value.shape
+    groups = lax.axis_size("space")
+    snaps = lax.axis_size("snap")
+    received = lax.all_to_all(partial_value, "space", 0, 0, tiled=True)
+    owned = jnp.sum(received, axis=0, keepdims=True)
+    spread = jnp.broadcast_to(owned, (groups * snaps, columns))
+    everyone = lax.all_to_all(spread, ("space", "snap"), 0, 0, tiled=True)
+    states = everyone.reshape(rank, columns * snaps)
     total_snaps = states.shape[1]
     feats = features_t(states)
     targets = (jnp.roll(states, -1, axis=1) - states).astype(jnp.bfloat16)
     width = feats.shape[0]
-    block_rows = width // lax.axis_size("snap")
+    block_rows = width // snaps
     chosen = lax.dynamic_slice_in_dim(feats, lax.axis_index("snap") * block_rows, block_rows, 0)
     dims = (((1,), (1,)), ((), ()))
     normal = lax.dot_general(chosen, feats, dims, preferred_element_type=jnp.float32) / total_snaps

time: 104 us -> 84 us (0.81)
  the two profiles are of different devices: /device:TPU:2 before, /device:TPU:1 now
where the time goes in v3:
time: 84 us; the launch traced here: 83.4 us
  blocking collectives  24.7 us (29%)
  waiting for transfers between devices  22.7 us (27%)
  matrix products  12 us (14%)
  starting transfers between devices  10.9 us (13%)
  Pallas kernels  7.35 us (9%)
  local copies, waits for them, and re-layouts  3.67 us (4%)
  other arithmetic  1.33 us (2%)
    all_to_all x1, blocking collectives, per_device(): received = lax.all_to_all(partial_value, 'space', 0, 0, tiled=True)  24.7 us
    all_to_all x1, waiting for transfers between devices, per_device(): everyone = lax.all_to_all(spread, ('space', 'snap'), 0, 0, tiled=True)  22.7 us
    all_to_all x1, starting transfers between devices, per_device(): everyone = lax.all_to_all(spread, ('space', 'snap'), 0, 0, tiled=True)  10.9 us
    dot_general x1, matrix products, per_device(): lax.dot_general(chosen, feats, dims, preferred_element_type=jnp.float32)  8.11 us
    pallas_call x1, Pallas kernels, features_t(): pl.pallas_call(feature_kernel, grid=(snaps // lanes,), in_specs=[pl.Block...  7.35 us
    dot_general x1, matrix products, per_device(): lax.dot_general(chosen, targets, dims, preferred_element_type=jnp.float32)  2.41 us
    unnamed x6, local copies, waits for them, and re-layouts  2.25 us
  transfers between devices with their start and end apart: 1, of which 1 were waited for; matrix products, arithmetic and copies ran while one was open for 0% of the time, Pallas kernels for 0%

profile of v3, /device:TPU:1, one launch (start us, length us, event | category | flops | bytes accessed | tf_op | source)
XLA Modules:
  0.0 83.4 jit_solution(5457168213857552948)
XLA Ops:
  0.6 0.0 copy-start
  0.6 1.6 %copy-done = bf16[4096,256]{1,0:T(8,128)(2,1)S(1)} copy-done((bf16[4096,256]{1,0:T(8,128)(2,1)S(1)}, bf16[4096,256]{1,0:T(8,128)(2,1)}, u32[]{:S(2)}) %copy-start) | copy-done | bytes 2097176
  2.2 1.5 %convolution_bitcast_fusion = f32[64,1,256]{2,0,1:T(8,128)S(1)} fusion(bf16[4096,64]{0,1:T(8,128)(2,1)} %param.3, bf16[4096,256]{1,0:T(8,128)(2,1)S(1)} %copy-done), kind=kOutput, calls=%fused_computation.2 | convolution fusion | flops 134217728 | bytes 2686976 | tf_op jit(solution)/shard_map/dot_general | solution.py:66
  3.7 0.1 copy.4
  3.8 24.7 %all_to_all.15 = f32[64,1,256]{2,1,0:T(1,128)S(1)} all-to-all(f32[64,1,256]{2,1,0:T(1,128)S(1)} %copy.4), channel_id=1, replica_groups=mesh['space'=64,'snap'=8] {'space'}, dimensions={0} | all-to-all | bytes 131072 | tf_op jit(solution)/shard_map/all_to_all | solution.py:72
  28.5 0.1 reduce_sum.9
  28.6 1.1 %broadcast_in_dim.2 = f32[512,1,256]{2,1,0:T(1,128)} broadcast(f32[256]{0:T(256)S(1)} %reduce_sum.9), dimensions={2} | broadcast | bytes 525312 | tf_op jit(solution)/shard_map/broadcast_in_dim | solution.py:74
  29.7 10.9 %all-to-all-start.1 = ((f32[512,1,256]{2,1,0:T(1,128)}), f32[512,1,256]{2,1,0:T(1,128)S(1)}, u32[]{:S(2)}, u32[]{:S(2)}) async-start(f32[512,1,256]{2,1,0:T(1,128)} %broadcast_in_dim.2), calls=%async_computation.1 | async-start | bytes 1048576 | tf_op jit(solution)/shard_map/all_to_all | solution.py:75
  40.6 22.7 %all-to-all-done.1 = f32[512,1,256]{2,1,0:T(1,128)S(1)} async-done(((f32[512,1,256]{2,1,0:T(1,128)}), f32[512,1,256]{2,1,0:T(1,128)S(1)}, u32[]{:S(2)}, u32[]{:S(2)}) %all-to-all-start.1) | async-done | bytes 524320 | tf_op jit(solution)/shard_map/all_to_all | solution.py:75
  63.3 1.2 %reduce.1 = f32[512,256]{1,0:T(8,128)S(1)} reduce(f32[512,1,256]{2,1,0:T(1,128)S(1)} %all-to-all-done.1, f32[]{:T(128)} %constant.17), dimensions={1}, to_apply=%all_to_all.12.reduce_sub_computation | reduce | bytes 1048580 | tf_op jit(solution)/shard_map/all_to_all | solution.py:75
  64.6 0.1 reshape.16.states_ref
  64.6 0.0 copy-start.1
  64.7 0.2 slice.10
  64.9 0.7 copy-done.1
  65.5 7.4 %shard_map.41 = bf16[2144,2048]{1,0:T(8,128)(2,1)} custom-call(f32[64,2048]{1,0:T(8,128)} %copy-done.1), custom_call_target="tpu_custom_call" | custom-call | flops 4390912 | bytes 9306112 | tf_op jit(solution)/shard_map/pallas_call | solution.py:52
  72.9 0.0 copy-start.2
  72.9 0.0 slice-start
  72.9 8.1 %convolution_multiply_fusion = f32[268,2144]{1,0:T(8,128)} fusion(bf16[2144,2048]{1,0:T(8,128)(2,1)} %shard_map.41, s32[]{:T(128)S(6)} %select_n.3), kind=kOutput, calls=%fused_computation | convolution fusion | flops 2354103296 | bytes 12194308 | tf_op jit(solution)/shard_map/dot_general | solution.py:84
  81.0 0.0 copy-done.2
  81.0 0.0 slice-done
  81.0 2.4 %convolution_multiply_fusion.1 = f32[268,64]{0,1:T(8,128)} fusion(bf16[2144,2048]{1,0:T(8,128)(2,1)} %shard_map.41, s32[]{:T(128)S(6)} %select_n.3, f32[64,2048]{1,0:T(8,128)S(1)} %copy-done.2, f32[64,1]{1,0:T(8,128)S(1)} %slice-done, f32[64,2047]{1,0:T(8,128)S(1)} %slice.10), kind=kOutput, calls=%fused_computation.1 | convolution fusion | flops 70664960 | bytes 2231300 | tf_op jit(solution)/shard_map/dot_general | solution.py:85
Async XLA Ops:
  0.6 1.6 %copy-start = (bf16[4096,256]{1,0:T(8,128)(2,1)S(1)}, bf16[4096,256]{1,0:T(8,128)(2,1)}, u32[]{:S(2)}) copy-start(bf16[4096,256]{1,0:T(8,128)(2,1)} %param.2) | copy-start | bytes 6291460
  29.7 33.6 %all-to-all-start.1 = ((f32[512,1,256]{2,1,0:T(1,128)}), f32[512,1,256]{2,1,0:T(1,128)S(1)}, u32[]{:S(2)}, u32[]{:S(2)}) async-start(f32[512,1,256]{2,1,0:T(1,128)} %broadcast_in_dim.2), calls=%async_computation.1 | async-start | bytes 1048576 | tf_op jit(solution)/shard_map/all_to_all | solution.py:75
  64.6 0.9 %copy-start.1 = (f32[64,2048]{1,0:T(8,128)}, f32[64,2048]{1,0:T(8,128)S(1)}, u32[]{:S(2)}) copy-start(f32[64,2048]{1,0:T(8,128)S(1)} %reshape.16.states_ref) | copy-start | bytes 1572868
  72.9 8.1 %copy-start.2 = (f32[64,2048]{1,0:T(8,128)S(1)}, f32[64,2048]{1,0:T(8,128)}, u32[]{:S(2)}) copy-start(f32[64,2048]{1,0:T(8,128)} %copy-done.1) | copy-start | bytes 1572868
  72.9 8.1 %slice-start = ((f32[64,2048]{1,0:T(8,128)}), f32[64,1]{1,0:T(8,128)S(1)}, s32[]{:S(2)}) async-start(f32[64,2048]{1,0:T(8,128)} %copy-done.1), calls=%async_computation.2 | async-start | bytes 65536 | tf_op jit(solution)/shard_map/jit(_roll_static)/slice | solution.py:79

commit v4 on v3

--- a/solution.py
+++ b/solution.py
@@ -71,8 +71,9 @@
     snaps = lax.axis_size("snap")
     received = lax.all_to_all(partial_value, "space", 0, 0, tiled=True)
     owned = jnp.sum(received, axis=0, keepdims=True)
-    spread = jnp.broadcast_to(owned, (groups * snaps, columns))
-    everyone = lax.all_to_all(spread, ("space", "snap"), 0, 0, tiled=True)
+    across = lax.all_to_all(jnp.broadcast_to(owned, (snaps, columns)), "snap", 0, 0, tiled=True)
+    row = across.reshape(1, snaps * columns)
+    everyone = lax.all_to_all(jnp.broadcast_to(row, (groups, snaps * columns)), "space", 0, 0, tiled=True)
     states = everyone.reshape(rank, columns * snaps)
     total_snaps = states.shape[1]
     feats = features_t(states)

time: 84 us -> 86.4 us (1.029)
  blocking collectives: 24.7 us -> 37.9 us
  starting transfers between devices: 10.9 us -> 5.89 us
  waiting for transfers between devices: 22.7 us -> 17.8 us
  other arithmetic: 1.33 us -> 0.1 us
    all_to_all x0 -> x1, blocking collectives: none -> 13.2 us  [per_device(): lax.all_to_all(jnp.broadcast_to(owned, (snaps, columns)), 'snap', 0, 0, t...]
    all_to_all x1, starting transfers between devices: 10.9 us -> 5.89 us  [per_device(): lax.all_to_all(jnp.broadcast_to(row, (groups, snaps * columns)), 'space',...]
    all_to_all x1, waiting for transfers between devices: 22.7 us -> 17.8 us  [per_device(): lax.all_to_all(jnp.broadcast_to(row, (groups, snaps * columns)), 'space',...]
    all_to_all x1 -> x0, other arithmetic: 1.24 us -> none  [per_device(): everyone = lax.all_to_all(spread, ('space', 'snap'), 0, 0, tiled=True)]
    unnamed x6 -> x7, local copies, waits for them, and re-layouts: 2.25 us -> 1.76 us
where the time goes in v4:
time: 86.4 us; the launch traced here: 85.7 us
  blocking collectives  37.9 us (44%)
  waiting for transfers between devices  17.8 us (21%)
  matrix products  12 us (14%)
  Pallas kernels  7.36 us (9%)
  starting transfers between devices  5.89 us (7%)
  local copies, waits for them, and re-layouts  3.97 us (5%)
    all_to_all x1, blocking collectives, per_device(): received = lax.all_to_all(partial_value, 'space', 0, 0, tiled=True)  24.7 us
    all_to_all x1, waiting for transfers between devices, per_device(): lax.all_to_all(jnp.broadcast_to(row, (groups, snaps * columns)), 'space',...  17.8 us
    all_to_all x1, blocking collectives, per_device(): lax.all_to_all(jnp.broadcast_to(owned, (snaps, columns)), 'snap', 0, 0, t...  13.2 us
    dot_general x1, matrix products, per_device(): lax.dot_general(chosen, feats, dims, preferred_element_type=jnp.float32)  8.11 us
    pallas_call x1, Pallas kernels, features_t(): pl.pallas_call(feature_kernel, grid=(snaps // lanes,), in_specs=[pl.Block...  7.36 us
    all_to_all x1, starting transfers between devices, per_device(): lax.all_to_all(jnp.broadcast_to(row, (groups, snaps * columns)), 'space',...  5.89 us
    dot_general x1, matrix products, per_device(): lax.dot_general(chosen, targets, dims, preferred_element_type=jnp.float32)  2.42 us
    unnamed x7, local copies, waits for them, and re-layouts  1.76 us
  transfers between devices with their start and end apart: 1, of which 1 were waited for; matrix products, arithmetic and copies ran while one was open for 0% of the time, Pallas kernels for 0%

profile of v4, /device:TPU:1, one launch (start us, length us, event | category | flops | bytes accessed | tf_op | source)
XLA Modules:
  0.0 85.7 jit_solution(2034716437103402574)
XLA Ops:
  0.6 0.0 copy-start
  0.6 1.6 %copy-done = bf16[4096,256]{1,0:T(8,128)(2,1)S(1)} copy-done((bf16[4096,256]{1,0:T(8,128)(2,1)S(1)}, bf16[4096,256]{1,0:T(8,128)(2,1)}, u32[]{:S(2)}) %copy-start) | copy-done | bytes 2097176
  2.2 1.5 %convolution_bitcast_fusion = f32[64,1,256]{2,0,1:T(8,128)S(1)} fusion(bf16[4096,64]{0,1:T(8,128)(2,1)} %param.3, bf16[4096,256]{1,0:T(8,128)(2,1)S(1)} %copy-done), kind=kOutput, calls=%fused_computation.2 | convolution fusion | flops 134217728 | bytes 2686976 | tf_op jit(solution)/shard_map/dot_general | solution.py:66
  3.7 0.1 copy.4
  3.8 24.7 %all_to_all.23 = f32[64,1,256]{2,1,0:T(1,128)S(1)} all-to-all(f32[64,1,256]{2,1,0:T(1,128)S(1)} %copy.4), channel_id=1, replica_groups=mesh['space'=64,'snap'=8] {'space'}, dimensions={0} | all-to-all | bytes 131072 | tf_op jit(solution)/shard_map/all_to_all | solution.py:72
  28.5 0.1 reduce_sum.9
  28.6 13.2 %all_to_all.24 = f32[8,1,256]{2,1,0:T(1,128)S(1)} all-to-all(f32[8,1,256]{2,1,0:T(1,128)S(1)} %broadcast_in_dim.6), channel_id=1, replica_groups=mesh['space'=64,'snap'=8] {'snap'}, dimensions={0} | all-to-all | bytes 16384 | tf_op jit(solution)/shard_map/all_to_all | solution.py:74
  41.8 1.1 %broadcast_in_dim.15 = f32[64,1,2048]{2,1,0:T(1,128)} broadcast(f32[2048]{0:T(1024)S(1)} %bitcast.15), dimensions={2} | broadcast | bytes 532480 | tf_op jit(solution)/shard_map/broadcast_in_dim | solution.py:76
  42.9 5.9 %all-to-all-start.2 = ((f32[64,1,2048]{2,1,0:T(1,128)}), f32[64,1,2048]{2,1,0:T(1,128)S(1)}, u32[]{:S(2)}, u32[]{:S(2)}) async-start(f32[64,1,2048]{2,1,0:T(1,128)} %broadcast_in_dim.15), calls=%async_computation.2 | async-start | bytes 1048576 | tf_op jit(solution)/shard_map/all_to_all | solution.py:76
  48.8 17.8 %all-to-all-done.2 = f32[64,1,2048]{2,1,0:T(1,128)S(1)} async-done(((f32[64,1,2048]{2,1,0:T(1,128)}), f32[64,1,2048]{2,1,0:T(1,128)S(1)}, u32[]{:S(2)}, u32[]{:S(2)}) %all-to-all-start.2) | async-done | bytes 524320 | tf_op jit(solution)/shard_map/all_to_all | solution.py:76
  66.6 0.2 copy.10
  66.8 0.0 copy-start.1
  66.8 1.1 %slice.10 = f32[64,2047]{1,0:T(8,128)} slice(f32[64,2048]{1,0:T(8,128)S(1)} %bitcast.13), slice={[0:64], [1:2048]} | slice | bytes 1048064 | tf_op jit(solution)/shard_map/jit(_roll_static)/slice | solution.py:80
  67.8 0.0 copy-done.1
  67.8 7.4 %shard_map.41 = bf16[2144,2048]{1,0:T(8,128)(2,1)} custom-call(f32[64,2048]{1,0:T(8,128)} %bitcast.14), custom_call_target="tpu_custom_call" | custom-call | flops 4390912 | bytes 9306112 | tf_op jit(solution)/shard_map/pallas_call | solution.py:52
  75.2 0.0 copy-start.2
  75.2 8.1 %convolution_multiply_fusion = f32[268,2144]{1,0:T(8,128)} fusion(bf16[2144,2048]{1,0:T(8,128)(2,1)} %shard_map.41, s32[]{:T(128)S(6)} %select_n.3), kind=kOutput, calls=%fused_computation | convolution fusion | flops 2354103296 | bytes 12194308 | tf_op jit(solution)/shard_map/dot_general | solution.py:85
  83.3 0.0 copy-done.2
  83.3 2.4 %convolution_multiply_fusion.1 = f32[268,64]{0,1:T(8,128)} fusion(bf16[2144,2048]{1,0:T(8,128)(2,1)} %shard_map.41, s32[]{:T(128)S(6)} %select_n.3, f32[64,1]{1,0:T(8,128)S(1)} %slice.11, f32[64,2047]{1,0:T(8,128)S(1)} %copy-done.2, f32[64,1,2048]{2,1,0:T(1,128)S(1)} %all-to-all-done.2), kind=kOutput, calls=%fused_computation.1 | convolution fusion | flops 70664960 | bytes 2231300 | tf_op jit(solution)/shard_map/dot_general | solution.py:86
  (2 shorter events, 0.0 us)
Async XLA Ops:
  0.6 1.6 %copy-start = (bf16[4096,256]{1,0:T(8,128)(2,1)S(1)}, bf16[4096,256]{1,0:T(8,128)(2,1)}, u32[]{:S(2)}) copy-start(bf16[4096,256]{1,0:T(8,128)(2,1)} %param.2) | copy-start | bytes 6291460
  42.9 23.7 %all-to-all-start.2 = ((f32[64,1,2048]{2,1,0:T(1,128)}), f32[64,1,2048]{2,1,0:T(1,128)S(1)}, u32[]{:S(2)}, u32[]{:S(2)}) async-start(f32[64,1,2048]{2,1,0:T(1,128)} %broadcast_in_dim.15), calls=%async_computation.2 | async-start | bytes 1048576 | tf_op jit(solution)/shard_map/all_to_all | solution.py:76
  66.8 1.1 %copy-start.1 = (f32[64,1,2048]{2,0,1:T(8,128)}, f32[64,1,2048]{2,0,1:T(8,128)S(1)}, u32[]{:S(2)}) copy-start(f32[64,1,2048]{2,0,1:T(8,128)S(1)} %copy.10) | copy-start | bytes 1572868
  75.2 8.1 %copy-start.2 = (f32[64,2047]{1,0:T(8,128)S(1)}, f32[64,2047]{1,0:T(8,128)}, u32[]{:S(2)}) copy-start(f32[64,2047]{1,0:T(8,128)} %slice.10) | copy-start | bytes 1572100

commit v5 on v3

--- a/solution.py
+++ b/solution.py
@@ -1,3 +1,5 @@
+import functools
+
 import jax
 import jax.numpy as jnp
 import numpy as np
@@ -35,7 +37,7 @@
     return block
 
 
-def feature_kernel(states_ref, out_ref, rows_ref):
+def fill_rows(states_ref, rows_ref):
     rank = states_ref.shape[0]
     rows_ref[0:rank, :] = states_ref[...]
     offset = rank
@@ -43,23 +45,61 @@
         count = rank - a
         rows_ref[offset : offset + count, :] = states_ref[a : a + 1, :] * states_ref[a:rank, :]
         offset += count
-    out_ref[...] = rows_ref[...].astype(out_ref.dtype)
 
 
-def features_t(states, lanes=256):
+def normal_kernel(first, count, scale, states_ref, targets_ref, normal_ref, rhs_ref, rows_ref):
+    step = pl.program_id(0)
+    fill_rows(states_ref, rows_ref)
+    feats = rows_ref[...].astype(jnp.bfloat16)
+    chosen = rows_ref[first : first + count, :].astype(jnp.bfloat16)
+    dims = (((1,), (1,)), ((), ()))
+    normal_part = lax.dot_general(chosen, feats, dims, preferred_element_type=jnp.float32)
+    rhs_part = lax.dot_general(chosen, targets_ref[...], dims, preferred_element_type=jnp.float32)
+
+    @pl.when(step == 0)
+    def _():
+        normal_ref[...] = normal_part
+        rhs_ref[...] = rhs_part
+
+    @pl.when(step > 0)
+    def _():
+        normal_ref[...] += normal_part
+        rhs_ref[...] += rhs_part
+
+    @pl.when(step == pl.num_programs(0) - 1)
+    def _():
+        normal_ref[...] = normal_ref[...] / scale
+        rhs_ref[...] = rhs_ref[...] / scale
+
+
+def normal_block(states, targets, block, blocks, lanes=256):
     rank, snaps = states.shape
     width = rank + rank * (rank + 1) // 2
+    count = width // blocks
+    kernel = functools.partial(normal_kernel, block * count, count, float(snaps))
     return pl.pallas_call(
-        feature_kernel,
+        kernel,
         grid=(snaps // lanes,),
-        in_specs=[pl.BlockSpec((rank, lanes), lambda j: (0, j))],
-        out_specs=pl.BlockSpec((width, lanes), lambda j: (0, j)),
-        out_shape=jax.ShapeDtypeStruct((width, snaps), jnp.bfloat16),
+        in_specs=[
+            pl.BlockSpec((rank, lanes), lambda j: (0, j)),
+            pl.BlockSpec((rank, lanes), lambda j: (0, j)),
+        ],
+        out_specs=[
+            pl.BlockSpec((count, width), lambda j: (0, 0)),
+            pl.BlockSpec((count, rank), lambda j: (0, 0)),
+        ],
+        out_shape=[
+            jax.ShapeDtypeStruct((count, width), jnp.float32),
+            jax.ShapeDtypeStruct((count, rank), jnp.float32),
+        ],
         scratch_shapes=[pltpu.VMEM((width, lanes), jnp.float32)],
+        compiler_params=pltpu.CompilerParams(vmem_limit_bytes=48 * 1024 * 1024),
         cost_estimate=pl.CostEstimate(
-            flops=width * snaps, transcendentals=0, bytes_accessed=rank * snaps * 4 + width * snaps * 2
+            flops=2 * count * (width + rank) * snaps,
+            transcendentals=0,
+            bytes_accessed=rank * snaps * 6 + count * (width + rank) * 4,
         ),
-    )(states)
+    )(states, targets)
 
 
 def per_device(snapshots, basis):
@@ -74,15 +114,9 @@
     spread = jnp.broadcast_to(owned, (groups * snaps, columns))
     everyone = lax.all_to_all(spread, ("space", "snap"), 0, 0, tiled=True)
     states = everyone.reshape(rank, columns * snaps)
-    total_snaps = states.shape[1]
-    feats = features_t(states)
     targets = (jnp.roll(states, -1, axis=1) - states).astype(jnp.bfloat16)
-    width = feats.shape[0]
-    block_rows = width // snaps
-    chosen = lax.dynamic_slice_in_dim(feats, lax.axis_index("snap") * block_rows, block_rows, 0)
-    dims = (((1,), (1,)), ((), ()))
-    normal = lax.dot_general(chosen, feats, dims, preferred_element_type=jnp.float32) / total_snaps
-    rhs = lax.dot_general(chosen, targets, dims, preferred_element_type=jnp.float32) / total_snaps
+    branches = [functools.partial(normal_block, block=b, blocks=snaps) for b in range(snaps)]
+    normal, rhs = lax.switch(lax.axis_index("snap"), branches, states, targets)
     return (normal, rhs)
 
 

time: 84 us -> 74.3 us (0.88)
  matrix products: 12 us -> 1.5 us
  Pallas kernels: 7.35 us -> 8.35 us
    dot_general x2 -> x0, matrix products: 10.5 us -> none  [the longest x1 8.11 us: per_device(): lax.dot_general(chosen, feats, dims, preferred_element_type=jnp.float32)]
    pallas_call x1, Pallas kernels: 7.35 us -> 8.35 us  [normal_block(): pl.pallas_call(kernel, grid=(snaps // lanes,), in_specs=[pl.BlockSpec((ra...]
    unnamed x6 -> x2, local copies, waits for them, and re-layouts: 2.25 us -> 1.59 us
where the time goes in v5:
time: 74.3 us; the launch traced here: 74.1 us
  blocking collectives  24.7 us (33%)
  waiting for transfers between devices  22.7 us (31%)
  starting transfers between devices  10.9 us (15%)
  Pallas kernels  8.35 us (11%)
  local copies, waits for them, and re-layouts  3.77 us (5%)
  matrix products  1.5 us (2%)
  other arithmetic  1.42 us (2%)
    all_to_all x1, blocking collectives, per_device(): received = lax.all_to_all(partial_value, 'space', 0, 0, tiled=True)  24.7 us
    all_to_all x1, waiting for transfers between devices, per_device(): everyone = lax.all_to_all(spread, ('space', 'snap'), 0, 0, tiled=True)  22.7 us
    all_to_all x1, starting transfers between devices, per_device(): everyone = lax.all_to_all(spread, ('space', 'snap'), 0, 0, tiled=True)  10.9 us
    pallas_call x1, Pallas kernels, normal_block(): pl.pallas_call(kernel, grid=(snaps // lanes,), in_specs=[pl.BlockSpec((ra...  8.35 us
    unnamed x2, local copies, waits for them, and re-layouts  1.59 us
    dot_general x1, matrix products, per_device(): lax.dot_general(basis, snapshots, (((0,), (0,)), ((), ())), preferred_ele...  1.5 us
  transfers between devices with their start and end apart: 1, of which 1 were waited for; matrix products, arithmetic and copies ran while one was open for 0% of the time, Pallas kernels for 0%

profile of v5, /device:TPU:1, one launch (start us, length us, event | category | flops | bytes accessed | tf_op | source)
XLA Modules:
  0.0 74.1 jit_solution(16680147657347205885)
XLA Ops:
  0.6 0.0 copy-start
  0.6 1.6 %copy-done = bf16[4096,256]{1,0:T(8,128)(2,1)S(1)} copy-done((bf16[4096,256]{1,0:T(8,128)(2,1)S(1)}, bf16[4096,256]{1,0:T(8,128)(2,1)}, u32[]{:S(2)}) %copy-start) | copy-done | bytes 2097176
  2.2 1.5 %convolution_bitcast_fusion = f32[64,1,256]{2,0,1:T(8,128)S(1)} fusion(bf16[4096,64]{0,1:T(8,128)(2,1)} %param.11, bf16[4096,256]{1,0:T(8,128)(2,1)S(1)} %copy-done), kind=kOutput, calls=%fused_computation | convolution fusion | flops 134217728 | bytes 2686976 | tf_op jit(solution)/shard_map/dot_general | solution.py:106
  3.7 0.1 copy.21
  3.8 24.7 %all_to_all.15 = f32[64,1,256]{2,1,0:T(1,128)S(1)} all-to-all(f32[64,1,256]{2,1,0:T(1,128)S(1)} %copy.21), channel_id=1, replica_groups=mesh['space'=64,'snap'=8] {'space'}, dimensions={0} | all-to-all | bytes 131072 | tf_op jit(solution)/shard_map/all_to_all | solution.py:112
  28.5 0.1 reduce_sum.9
  28.6 1.1 %broadcast_in_dim.2 = f32[512,1,256]{2,1,0:T(1,128)} broadcast(f32[256]{0:T(256)S(1)} %reduce_sum.9), dimensions={2} | broadcast | bytes 525312 | tf_op jit(solution)/shard_map/broadcast_in_dim | solution.py:114
  29.7 10.9 %all-to-all-start.1 = ((f32[512,1,256]{2,1,0:T(1,128)}), f32[512,1,256]{2,1,0:T(1,128)S(1)}, u32[]{:S(2)}, u32[]{:S(2)}) async-start(f32[512,1,256]{2,1,0:T(1,128)} %broadcast_in_dim.2), calls=%async_computation.1 | async-start | bytes 1048576 | tf_op jit(solution)/shard_map/all_to_all | solution.py:115
  40.6 22.7 %all-to-all-done.1 = f32[512,1,256]{2,1,0:T(1,128)S(1)} async-done(((f32[512,1,256]{2,1,0:T(1,128)}), f32[512,1,256]{2,1,0:T(1,128)S(1)}, u32[]{:S(2)}, u32[]{:S(2)}) %all-to-all-start.1) | async-done | bytes 524320 | tf_op jit(solution)/shard_map/all_to_all | solution.py:115
  63.3 1.2 %reduce.1 = f32[512,256]{1,0:T(8,128)S(1)} reduce(f32[512,1,256]{2,1,0:T(1,128)S(1)} %all-to-all-done.1, f32[]{:T(128)} %constant.10), dimensions={1}, to_apply=%all_to_all.12.reduce_sub_computation | reduce | bytes 1048580 | tf_op jit(solution)/shard_map/all_to_all | solution.py:115
  64.6 0.1 reshape.16
  64.7 0.2 slice.10
  64.9 0.1 fusion
  65.0 9.1 %conditional.1 = (f32[268,2144]{1,0:T(8,128)}, f32[268,64]{0,1:T(8,128)}) conditional(s32[]{:T(128)} %clamp.3, (f32[64,2048]{1,0:T(8,128)S(1)}, bf16[64,2048]{1,0:T(8,128)(2,1)S(1)}) %tuple.31, (f32[64,2048]{1,0:T(8,128)S(1)}, bf16[64,2048]{1,0:T(8,128)(2,1)S(1)}) %tuple.31, (f32[64,2048]{1,0:T(8,128)S(1)}, ...), branch_computations={%region_1.2_spmd, %region_2.3_spmd, %region_3.4_spmd, %region_4.5_... | conditional | flops 2423783424 | bytes 3290640 | solution.py:119
  65.0 8.4 %branch_0_fun.1 = (f32[268,2144]{1,0:T(8,128)}, f32[268,64]{1,0:T(8,128)S(1)}) custom-call(f32[64,2048]{1,0:T(8,128)S(1)} %get-tuple-element.32.states_ref, bf16[64,2048]{1,0:T(8,128)(2,1)S(1)} %get-tuple-element.33.targets_ref), custom_call_target="tpu_custom_call" | custom-call | flops 2423783424 | bytes 3153408 | tf_op jit(solution)/shard_map/cond/branch_0_fun/pallas_call | solution.py:80
  73.3 0.8 %copy.23 = f32[268,64]{0,1:T(8,128)} copy(f32[268,64]{1,0:T(8,128)S(1)} %get-tuple-element.73) | data formatting | bytes 137216 | tf_op jit(solution)/shard_map/cond | solution.py:119
  (1 shorter events, 0.0 us)
Async XLA Ops:
  0.6 1.6 %copy-start = (bf16[4096,256]{1,0:T(8,128)(2,1)S(1)}, bf16[4096,256]{1,0:T(8,128)(2,1)}, u32[]{:S(2)}) copy-start(bf16[4096,256]{1,0:T(8,128)(2,1)} %param.10) | copy-start | bytes 6291460
  29.7 33.6 %all-to-all-start.1 = ((f32[512,1,256]{2,1,0:T(1,128)}), f32[512,1,256]{2,1,0:T(1,128)S(1)}, u32[]{:S(2)}, u32[]{:S(2)}) async-start(f32[512,1,256]{2,1,0:T(1,128)} %broadcast_in_dim.2), calls=%async_computation.1 | async-start | bytes 1048576 | tf_op jit(solution)/shard_map/all_to_all | solution.py:115

commit v6 on v5

--- a/solution.py
+++ b/solution.py
@@ -72,7 +72,7 @@
         rhs_ref[...] = rhs_ref[...] / scale
 
 
-def normal_block(states, targets, block, blocks, lanes=256):
+def normal_block(states, targets, block, blocks, lanes=1024):
     rank, snaps = states.shape
     width = rank + rank * (rank + 1) // 2
     count = width // blocks

time: 74.3 us -> 71.6 us (0.964)
  Pallas kernels: 8.35 us -> 5.56 us
    pallas_call x1, Pallas kernels: 8.35 us -> 5.56 us  [normal_block(): pl.pallas_call(kernel, grid=(snaps // lanes,), in_specs=[pl.BlockSpec((ra...]
where the time goes in v6:
time: 71.6 us; the launch traced here: 71.3 us
  blocking collectives  24.7 us (34%)
  waiting for transfers between devices  22.7 us (32%)
  starting transfers between devices  10.9 us (15%)
  Pallas kernels  5.56 us (8%)
  local copies, waits for them, and re-layouts  3.77 us (5%)
  matrix products  1.51 us (2%)
  other arithmetic  1.42 us (2%)
    all_to_all x1, blocking collectives, per_device(): received = lax.all_to_all(partial_value, 'space', 0, 0, tiled=True)  24.7 us
    all_to_all x1, waiting for transfers between devices, per_device(): everyone = lax.all_to_all(spread, ('space', 'snap'), 0, 0, tiled=True)  22.7 us
    all_to_all x1, starting transfers between devices, per_device(): everyone = lax.all_to_all(spread, ('space', 'snap'), 0, 0, tiled=True)  10.9 us
    pallas_call x1, Pallas kernels, normal_block(): pl.pallas_call(kernel, grid=(snaps // lanes,), in_specs=[pl.BlockSpec((ra...  5.56 us
    unnamed x2, local copies, waits for them, and re-layouts  1.59 us
    dot_general x1, matrix products, per_device(): lax.dot_general(basis, snapshots, (((0,), (0,)), ((), ())), preferred_ele...  1.51 us
  transfers between devices with their start and end apart: 1, of which 1 were waited for; matrix products, arithmetic and copies ran while one was open for 0% of the time, Pallas kernels for 0%

profile of v6, /device:TPU:1, one launch (start us, length us, event | category | flops | bytes accessed | tf_op | source)
XLA Modules:
  0.0 71.3 jit_solution(6744357726455948384)
XLA Ops:
  0.6 0.0 copy-start
  0.6 1.6 %copy-done = bf16[4096,256]{1,0:T(8,128)(2,1)S(1)} copy-done((bf16[4096,256]{1,0:T(8,128)(2,1)S(1)}, bf16[4096,256]{1,0:T(8,128)(2,1)}, u32[]{:S(2)}) %copy-start) | copy-done | bytes 2097176
  2.2 1.5 %convolution_bitcast_fusion = f32[64,1,256]{2,0,1:T(8,128)S(1)} fusion(bf16[4096,64]{0,1:T(8,128)(2,1)} %param.11, bf16[4096,256]{1,0:T(8,128)(2,1)S(1)} %copy-done), kind=kOutput, calls=%fused_computation | convolution fusion | flops 134217728 | bytes 2686976 | tf_op jit(solution)/shard_map/dot_general | solution.py:106
  3.7 0.1 copy.21
  3.8 24.7 %all_to_all.15 = f32[64,1,256]{2,1,0:T(1,128)S(1)} all-to-all(f32[64,1,256]{2,1,0:T(1,128)S(1)} %copy.21), channel_id=1, replica_groups=mesh['space'=64,'snap'=8] {'space'}, dimensions={0} | all-to-all | bytes 131072 | tf_op jit(solution)/shard_map/all_to_all | solution.py:112
  28.5 0.1 reduce_sum.9
  28.6 1.1 %broadcast_in_dim.2 = f32[512,1,256]{2,1,0:T(1,128)} broadcast(f32[256]{0:T(256)S(1)} %reduce_sum.9), dimensions={2} | broadcast | bytes 525312 | tf_op jit(solution)/shard_map/broadcast_in_dim | solution.py:114
  29.7 10.9 %all-to-all-start.1 = ((f32[512,1,256]{2,1,0:T(1,128)}), f32[512,1,256]{2,1,0:T(1,128)S(1)}, u32[]{:S(2)}, u32[]{:S(2)}) async-start(f32[512,1,256]{2,1,0:T(1,128)} %broadcast_in_dim.2), calls=%async_computation.1 | async-start | bytes 1048576 | tf_op jit(solution)/shard_map/all_to_all | solution.py:115
  40.6 22.7 %all-to-all-done.1 = f32[512,1,256]{2,1,0:T(1,128)S(1)} async-done(((f32[512,1,256]{2,1,0:T(1,128)}), f32[512,1,256]{2,1,0:T(1,128)S(1)}, u32[]{:S(2)}, u32[]{:S(2)}) %all-to-all-start.1) | async-done | bytes 524320 | tf_op jit(solution)/shard_map/all_to_all | solution.py:115
  63.3 1.2 %reduce.1 = f32[512,256]{1,0:T(8,128)S(1)} reduce(f32[512,1,256]{2,1,0:T(1,128)S(1)} %all-to-all-done.1, f32[]{:T(128)} %constant.10), dimensions={1}, to_apply=%all_to_all.12.reduce_sub_computation | reduce | bytes 1048580 | tf_op jit(solution)/shard_map/all_to_all | solution.py:115
  64.6 0.1 reshape.16
  64.7 0.2 slice.10
  64.9 0.1 fusion
  65.0 6.3 %conditional.1 = (f32[268,2144]{1,0:T(8,128)}, f32[268,64]{0,1:T(8,128)}) conditional(s32[]{:T(128)} %clamp.3, (f32[64,2048]{1,0:T(8,128)S(1)}, bf16[64,2048]{1,0:T(8,128)(2,1)S(1)}) %tuple.31, (f32[64,2048]{1,0:T(8,128)S(1)}, bf16[64,2048]{1,0:T(8,128)(2,1)S(1)}) %tuple.31, (f32[64,2048]{1,0:T(8,128)S(1)}, ...), branch_computations={%region_1.2_spmd, %region_2.3_spmd, %region_3.4_spmd, %region_4.5_... | conditional | flops 2423783424 | bytes 3290640 | solution.py:119
  65.0 5.6 %branch_0_fun.1 = (f32[268,2144]{1,0:T(8,128)}, f32[268,64]{1,0:T(8,128)S(1)}) custom-call(f32[64,2048]{1,0:T(8,128)S(1)} %get-tuple-element.32.states_ref, bf16[64,2048]{1,0:T(8,128)(2,1)S(1)} %get-tuple-element.33.targets_ref), custom_call_target="tpu_custom_call" | custom-call | flops 2423783424 | bytes 3153408 | tf_op jit(solution)/shard_map/cond/branch_0_fun/pallas_call | solution.py:80
  70.5 0.8 %copy.23 = f32[268,64]{0,1:T(8,128)} copy(f32[268,64]{1,0:T(8,128)S(1)} %get-tuple-element.73) | data formatting | bytes 137216 | tf_op jit(solution)/shard_map/cond | solution.py:119
  (1 shorter events, 0.0 us)
Async XLA Ops:
  0.6 1.6 %copy-start = (bf16[4096,256]{1,0:T(8,128)(2,1)S(1)}, bf16[4096,256]{1,0:T(8,128)(2,1)}, u32[]{:S(2)}) copy-start(bf16[4096,256]{1,0:T(8,128)(2,1)} %param.10) | copy-start | bytes 6291460
  29.7 33.6 %all-to-all-start.1 = ((f32[512,1,256]{2,1,0:T(1,128)}), f32[512,1,256]{2,1,0:T(1,128)S(1)}, u32[]{:S(2)}, u32[]{:S(2)}) async-start(f32[512,1,256]{2,1,0:T(1,128)} %broadcast_in_dim.2), calls=%async_computation.1 | async-start | bytes 1048576 | tf_op jit(solution)/shard_map/all_to_all | solution.py:115

commit v7 on v6

--- a/solution.py
+++ b/solution.py
@@ -107,13 +107,21 @@
         basis, snapshots, (((0,), (0,)), ((), ())), preferred_element_type=jnp.float32
     )
     rank, columns = partial_value.shape
-    groups = lax.axis_size("space")
+    chips = lax.axis_size("chip")
+    cores = lax.axis_size("core")
     snaps = lax.axis_size("snap")
-    received = lax.all_to_all(partial_value, "space", 0, 0, tiled=True)
+    core = lax.axis_index("core")
+    by_chip = partial_value.reshape(cores, chips, columns).transpose(1, 0, 2).reshape(rank, columns)
+    received = lax.all_to_all(by_chip, ("chip", "core"), 0, 0, tiled=True)
     owned = jnp.sum(received, axis=0, keepdims=True)
-    spread = jnp.broadcast_to(owned, (groups * snaps, columns))
-    everyone = lax.all_to_all(spread, ("space", "snap"), 0, 0, tiled=True)
-    states = everyone.reshape(rank, columns * snaps)
+    spread = jnp.broadcast_to(owned, (chips * snaps, columns))
+    half = lax.all_to_all(spread, ("chip", "snap"), 0, 0, tiled=True).reshape(chips, snaps * columns)
+    other = lax.ppermute(half, "core", [(0, 1), (1, 0)])
+    states = jnp.where(
+        core == 0,
+        jnp.concatenate([half, other], axis=0),
+        jnp.concatenate([other, half], axis=0),
+    )
     targets = (jnp.roll(states, -1, axis=1) - states).astype(jnp.bfloat16)
     branches = [functools.partial(normal_block, block=b, blocks=snaps) for b in range(snaps)]
     normal, rhs = lax.switch(lax.axis_index("snap"), branches, states, targets)
@@ -121,10 +129,14 @@
 
 
 def solution(mesh):
+    space, snaps = mesh.devices.shape
+    chip_mesh = jax.sharding.Mesh(
+        mesh.devices.reshape(space // 2, 2, snaps), ("chip", "core", mesh.axis_names[1])
+    )
     return jax.shard_map(
         per_device,
-        mesh=mesh,
-        in_specs=(P("space", "snap"), P("space", None)),
+        mesh=chip_mesh,
+        in_specs=(P(("chip", "core"), "snap"), P(("chip", "core"), None)),
         out_specs=(P("snap", None), P("snap", None)),
         check_vma=False,
     )

time: 71.6 us -> 68.1 us (0.951)
  blocking collectives: 24.7 us -> 51.2 us
  waiting for transfers between devices: 22.7 us -> 1.13 us
  starting transfers between devices: 10.9 us -> 3.99 us
  local copies, waits for them, and re-layouts: 3.77 us -> 2.89 us
    all_to_all x1 -> x2, blocking collectives: 24.7 us -> 51.2 us  [the longest x1 26.5 us: per_device(): lax.all_to_all(spread, ('chip', 'snap'), 0, 0, tiled=True)]
    all_to_all x1 -> x0, waiting for transfers between devices: 22.7 us -> none  [per_device(): everyone = lax.all_to_all(spread, ('space', 'snap'), 0, 0, tiled=True)]
    all_to_all x1 -> x0, starting transfers between devices: 10.9 us -> none  [per_device(): everyone = lax.all_to_all(spread, ('space', 'snap'), 0, 0, tiled=True)]
    ppermute x0 -> x1, starting transfers between devices: none -> 3.99 us  [per_device(): other = lax.ppermute(half, 'core', [(0, 1), (1, 0)])]
    ppermute x0 -> x1, waiting for transfers between devices: none -> 1.13 us  [per_device(): other = lax.ppermute(half, 'core', [(0, 1), (1, 0)])]
    broadcast_in_dim x1, local copies, waits for them, and re-layouts: 1.07 us -> 0.14 us  [per_device(): spread = jnp.broadcast_to(owned, (chips * snaps, columns))]
where the time goes in v7:
time: 68.1 us; the launch traced here: 67.8 us
  blocking collectives  51.2 us (75%)
  Pallas kernels  5.56 us (8%)
  starting transfers between devices  3.99 us (6%)
  local copies, waits for them, and re-layouts  2.89 us (4%)
  matrix products  1.51 us (2%)
  waiting for transfers between devices  1.13 us (2%)
  other arithmetic  0.83 us (1%)
  between operations  0.7 us (1%)
    all_to_all x1, blocking collectives, per_device(): lax.all_to_all(spread, ('chip', 'snap'), 0, 0, tiled=True)  26.5 us
    all_to_all x1, blocking collectives, per_device(): received = lax.all_to_all(by_chip, ('chip', 'core'), 0, 0, tiled=True)  24.7 us
    pallas_call x1, Pallas kernels, normal_block(): pl.pallas_call(kernel, grid=(snaps // lanes,), in_specs=[pl.BlockSpec((ra...  5.56 us
    ppermute x1, starting transfers between devices, per_device(): other = lax.ppermute(half, 'core', [(0, 1), (1, 0)])  3.99 us
    unnamed x2, local copies, waits for them, and re-layouts  1.59 us
    dot_general x1, matrix products, per_device(): lax.dot_general(basis, snapshots, (((0,), (0,)), ((), ())), preferred_ele...  1.51 us
  transfers between devices with their start and end apart: 1, of which 1 were waited for; matrix products, arithmetic and copies ran while one was open for 0% of the time, Pallas kernels for 0%

profile of v7, /device:TPU:1, one launch (start us, length us, event | category | flops | bytes accessed | tf_op | source)
XLA Modules:
  0.0 67.8 jit_solution(3432348273052573304)
XLA Ops:
  0.6 0.0 copy-start
  0.6 1.6 %copy-done = bf16[4096,256]{1,0:T(8,128)(2,1)S(1)} copy-done((bf16[4096,256]{1,0:T(8,128)(2,1)S(1)}, bf16[4096,256]{1,0:T(8,128)(2,1)}, u32[]{:S(2)}) %copy-start) | copy-done | bytes 2097176
  2.2 1.5 %fusion.1 = f32[64,256]{1,0:T(8,128)S(1)} fusion(bf16[4096,64]{0,1:T(8,128)(2,1)} %param.11, bf16[4096,256]{1,0:T(8,128)(2,1)S(1)} %copy-done), kind=kOutput, calls=%fused_computation.4 | convolution fusion | flops 134217728 | bytes 2686976 | tf_op jit(solution)/shard_map/dot_general | solution.py:106
  3.7 0.1 copy.35
  3.8 0.1 all_to_all.13
  3.9 24.7 %all_to_all.16 = f32[64,1,256]{2,1,0:T(1,128)S(1)} all-to-all(f32[64,1,256]{2,1,0:T(1,128)S(1)} %all_to_all.13), channel_id=1, replica_groups=mesh['chip'=32,'core'=2,'snap'=8] {'chip','core'}, dimensions={0} | all-to-all | bytes 131072 | tf_op jit(solution)/shard_map/all_to_all | solution.py:115
  28.6 0.1 reduce_sum.9
  28.7 0.1 broadcast_in_dim.2
  28.9 26.5 %all_to_all.17 = f32[256,1,256]{2,1,0:T(1,128)S(1)} all-to-all(f32[256,1,256]{2,1,0:T(1,128)S(1)} %broadcast_in_dim.2), channel_id=1, replica_groups=mesh['chip'=32,'core'=2,'snap'=8] {'chip','snap'}, dimensions={0} | all-to-all | bytes 524288 | tf_op jit(solution)/shard_map/all_to_all | solution.py:118
  55.3 0.6 reduce.1
  56.0 4.0 %collective-permute-start = (f32[32,2048]{1,0:T(8,128)S(1)}, f32[32,2048]{1,0:T(8,128)S(1)}, u32[]{:S(2)}, u32[]{:S(2)}) collective-permute-start(f32[32,2048]{1,0:T(8,128)S(1)} %reshape.22), channel_id=1, source_target_pairs={{0,8},{8,0},{1,9},{9,1},{2,10},{10,2},{3,11},{11,3},{4,12},{12,4},... | collective-permute-start | bytes 786440 | tf_op jit(solution)/shard_map/ppermute | solution.py:119
  60.0 1.1 %collective-permute-done = f32[32,2048]{1,0:T(8,128)S(1)} collective-permute-done((f32[32,2048]{1,0:T(8,128)S(1)}, f32[32,2048]{1,0:T(8,128)S(1)}, u32[]{:S(2)}, u32[]{:S(2)}) %collective-permute-start) | collective-permute-done | bytes 262176 | tf_op jit(solution)/shard_map/ppermute | solution.py:119
  61.2 0.2 slice.10
  61.4 0.1 fusion
  61.5 6.3 %conditional.1 = (f32[268,2144]{1,0:T(8,128)}, f32[268,64]{0,1:T(8,128)}) conditional(s32[]{:T(128)} %clamp.3, (f32[64,2048]{1,0:T(8,128)S(1)}, bf16[64,2048]{1,0:T(8,128)(2,1)S(1)}) %tuple.31, (f32[64,2048]{1,0:T(8,128)S(1)}, bf16[64,2048]{1,0:T(8,128)(2,1)S(1)}) %tuple.31, (f32[64,2048]{1,0:T(8,128)S(1)}, ...), branch_computations={%region_1.2_spmd, %region_2.3_spmd, %region_3.4_spmd, %region_4.5_... | conditional | flops 2423783424 | bytes 3290640 | solution.py:127
  61.5 5.6 %branch_0_fun.1 = (f32[268,2144]{1,0:T(8,128)}, f32[268,64]{1,0:T(8,128)S(1)}) custom-call(f32[64,2048]{1,0:T(8,128)S(1)} %get-tuple-element.32.states_ref, bf16[64,2048]{1,0:T(8,128)(2,1)S(1)} %get-tuple-element.33.targets_ref), custom_call_target="tpu_custom_call" | custom-call | flops 2423783424 | bytes 3153408 | tf_op jit(solution)/shard_map/cond/branch_0_fun/pallas_call | solution.py:80
  67.0 0.8 %copy.26 = f32[268,64]{0,1:T(8,128)} copy(f32[268,64]{1,0:T(8,128)S(1)} %get-tuple-element.75) | data formatting | bytes 137216 | tf_op jit(solution)/shard_map/cond | solution.py:127
  (3 shorter events, 0.1 us)
Async XLA Ops:
  0.6 1.6 %copy-start = (bf16[4096,256]{1,0:T(8,128)(2,1)S(1)}, bf16[4096,256]{1,0:T(8,128)(2,1)}, u32[]{:S(2)}) copy-start(bf16[4096,256]{1,0:T(8,128)(2,1)} %param.10) | copy-start | bytes 6291460
  56.0 5.1 %collective-permute-start = (f32[32,2048]{1,0:T(8,128)S(1)}, f32[32,2048]{1,0:T(8,128)S(1)}, u32[]{:S(2)}, u32[]{:S(2)}) collective-permute-start(f32[32,2048]{1,0:T(8,128)S(1)} %reshape.22), channel_id=1, source_target_pairs={{0,8},{8,0},{1,9},{9,1},{2,10},{10,2},{3,11},{11,3},{4,12},{12,4},... | collective-permute-start | bytes 786440 | tf_op jit(solution)/shard_map/ppermute | solution.py:119

commit v8 on v7

--- a/solution.py
+++ b/solution.py
@@ -72,7 +72,7 @@
         rhs_ref[...] = rhs_ref[...] / scale
 
 
-def normal_block(states, targets, block, blocks, lanes=1024):
+def normal_block(states, targets, block, blocks, lanes=2048):
     rank, snaps = states.shape
     width = rank + rank * (rank + 1) // 2
     count = width // blocks
@@ -102,10 +102,42 @@
     )(states, targets)
 
 
+def project_kernel(basis_ref, snapshots_ref, out_ref):
+    part = lax.dot_general(
+        basis_ref[...], snapshots_ref[...], (((0,), (0,)), ((), ())), preferred_element_type=jnp.float32
+    )
+
+    @pl.when(pl.program_id(0) == 0)
+    def _():
+        out_ref[...] = part
+
+    @pl.when(pl.program_id(0) > 0)
+    def _():
+        out_ref[...] += part
+
+
+def project(basis, snapshots, depth=512):
+    rows, rank = basis.shape
+    columns = snapshots.shape[1]
+    return pl.pallas_call(
+        project_kernel,
+        grid=(rows // depth,),
+        in_specs=[
+            pl.BlockSpec((depth, rank), lambda k: (k, 0)),
+            pl.BlockSpec((depth, columns), lambda k: (k, 0)),
+        ],
+        out_specs=pl.BlockSpec((rank, columns), lambda k: (0, 0)),
+        out_shape=jax.ShapeDtypeStruct((rank, columns), jnp.float32),
+        cost_estimate=pl.CostEstimate(
+            flops=2 * rows * rank * columns,
+            transcendentals=0,
+            bytes_accessed=rows * (rank + columns) * 2 + rank * columns * 4,
+        ),
+    )(basis, snapshots)
+
+
 def per_device(snapshots, basis):
-    partial_value = lax.dot_general(
-        basis, snapshots, (((0,), (0,)), ((), ())), preferred_element_type=jnp.float32
-    )
+    partial_value = project(basis, snapshots)
     rank, columns = partial_value.shape
     chips = lax.axis_size("chip")
     cores = lax.axis_size("core")

time: 68.1 us -> 74.1 us (1.088)
  Pallas kernels: 5.56 us -> 10.8 us
  local copies, waits for them, and re-layouts: 2.89 us -> 4.5 us
  matrix products: 1.51 us -> 0 us
    pallas_call x0 -> x1, Pallas kernels: none -> 5.88 us  [project(): pl.pallas_call(project_kernel, grid=(rows // depth,), in_specs=[pl.BlockS...]
    dot_general x1 -> x0, matrix products: 1.51 us -> none  [per_device(): lax.dot_general(basis, snapshots, (((0,), (0,)), ((), ())), preferred_ele...]
    reshape x1, local copies, waits for them, and re-layouts: 0.05 us -> 0.89 us  [per_device(): partial_value.reshape(cores, chips, columns).transpose(1, 0, 2)]
    unnamed x2 -> x1, local copies, waits for them, and re-layouts: 1.59 us -> 2.36 us
where the time goes in v8:
time: 74.1 us; the launch traced here: 73.7 us
  blocking collectives  51.2 us (69%)
  Pallas kernels  10.8 us (15%)
  local copies, waits for them, and re-layouts  4.5 us (6%)
  starting transfers between devices  3.99 us (5%)
  waiting for transfers between devices  1.13 us (2%)
  between operations  0.93 us (1%)
  other arithmetic  0.83 us (1%)
    all_to_all x1, blocking collectives, per_device(): lax.all_to_all(spread, ('chip', 'snap'), 0, 0, tiled=True)  26.5 us
    all_to_all x1, blocking collectives, per_device(): received = lax.all_to_all(by_chip, ('chip', 'core'), 0, 0, tiled=True)  24.7 us
    pallas_call x1, Pallas kernels, project(): pl.pallas_call(project_kernel, grid=(rows // depth,), in_specs=[pl.BlockS...  5.88 us
    pallas_call x1, Pallas kernels, normal_block(): pl.pallas_call(kernel, grid=(snaps // lanes,), in_specs=[pl.BlockSpec((ra...  4.89 us
    ppermute x1, starting transfers between devices, per_device(): other = lax.ppermute(half, 'core', [(0, 1), (1, 0)])  3.99 us
    unnamed x1, local copies, waits for them, and re-layouts  2.36 us
  transfers between devices with their start and end apart: 1, of which 1 were waited for; matrix products, arithmetic and copies ran while one was open for 0% of the time, Pallas kernels for 0%

profile of v8, /device:TPU:1, one launch (start us, length us, event | category | flops | bytes accessed | tf_op | source)
XLA Modules:
  0.0 73.7 jit_solution(17404405671648731441)
XLA Ops:
  0.6 2.4 %copy.25.basis_ref = bf16[4096,64]{1,0:T(8,128)(2,1)} copy(bf16[4096,64]{0,1:T(8,128)(2,1)} %param.11) | data formatting | bytes 1048576 | tf_op args[1]
  3.0 5.9 %shard_map.57 = f32[64,256]{1,0:T(8,128)} custom-call(bf16[4096,64]{1,0:T(8,128)(2,1)} %copy.25.basis_ref, bf16[4096,256]{1,0:T(8,128)(2,1)} %snapshots_ref.1), custom_call_target="tpu_custom_call" | custom-call | flops 134217728 | bytes 2686976 | tf_op jit(solution)/shard_map/pallas_call | solution.py:122
  8.9 0.9 %copy.38 = f32[2,32,256]{2,0,1:T(2,128)S(1)} copy(f32[2,32,256]{2,1,0:T(8,128)} %bitcast.4) | data formatting | bytes 131072 | tf_op jit(solution)/shard_map/reshape | solution.py:146
  9.8 0.1 all_to_all.13
  9.9 24.7 %all_to_all.16 = f32[64,1,256]{2,1,0:T(1,128)S(1)} all-to-all(f32[64,1,256]{2,1,0:T(1,128)S(1)} %all_to_all.13), channel_id=1, replica_groups=mesh['chip'=32,'core'=2,'snap'=8] {'chip','core'}, dimensions={0} | all-to-all | bytes 131072 | tf_op jit(solution)/shard_map/all_to_all | solution.py:147
  34.6 0.1 reduce_sum.9
  34.7 0.1 broadcast_in_dim.2
  34.8 26.5 %all_to_all.17 = f32[256,1,256]{2,1,0:T(1,128)S(1)} all-to-all(f32[256,1,256]{2,1,0:T(1,128)S(1)} %broadcast_in_dim.2), channel_id=1, replica_groups=mesh['chip'=32,'core'=2,'snap'=8] {'chip','snap'}, dimensions={0} | all-to-all | bytes 524288 | tf_op jit(solution)/shard_map/all_to_all | solution.py:150
  61.3 0.6 reduce.1
  62.0 4.0 %collective-permute-start = (f32[32,2048]{1,0:T(8,128)S(1)}, f32[32,2048]{1,0:T(8,128)S(1)}, u32[]{:S(2)}, u32[]{:S(2)}) collective-permute-start(f32[32,2048]{1,0:T(8,128)S(1)} %reshape.22), channel_id=1, source_target_pairs={{0,8},{8,0},{1,9},{9,1},{2,10},{10,2},{3,11},{11,3},{4,12},{12,4},... | collective-permute-start | bytes 786440 | tf_op jit(solution)/shard_map/ppermute | solution.py:151
  66.0 1.1 %collective-permute-done = f32[32,2048]{1,0:T(8,128)S(1)} collective-permute-done((f32[32,2048]{1,0:T(8,128)S(1)}, f32[32,2048]{1,0:T(8,128)S(1)}, u32[]{:S(2)}, u32[]{:S(2)}) %collective-permute-start) | collective-permute-done | bytes 262176 | tf_op jit(solution)/shard_map/ppermute | solution.py:151
  67.1 0.2 slice.10
  67.3 0.1 fusion
  67.4 6.0 %conditional.1 = (f32[268,2144]{1,0:T(8,128)}, f32[268,64]{0,1:T(8,128)}) conditional(s32[]{:T(128)} %clamp.3, (f32[64,2048]{1,0:T(8,128)S(1)}, bf16[64,2048]{1,0:T(8,128)(2,1)S(1)}) %tuple.31, (f32[64,2048]{1,0:T(8,128)S(1)}, bf16[64,2048]{1,0:T(8,128)(2,1)S(1)}) %tuple.31, (f32[64,2048]{1,0:T(8,128)S(1)}, ...), branch_computations={%region_1.2_spmd, %region_2.3_spmd, %region_3.4_spmd, %region_4.5_... | conditional | flops 2423783424 | bytes 3290640 | solution.py:159
  67.5 4.9 %branch_0_fun.1 = (f32[268,2144]{1,0:T(8,128)}, f32[268,64]{1,0:T(8,128)S(1)}) custom-call(f32[64,2048]{1,0:T(8,128)S(1)} %get-tuple-element.32.states_ref, bf16[64,2048]{1,0:T(8,128)(2,1)S(1)} %get-tuple-element.33.targets_ref), custom_call_target="tpu_custom_call" | custom-call | flops 2423783424 | bytes 3153408 | tf_op jit(solution)/shard_map/cond/branch_0_fun/pallas_call | solution.py:80
  72.3 0.8 %copy.29 = f32[268,64]{0,1:T(8,128)} copy(f32[268,64]{1,0:T(8,128)S(1)} %get-tuple-element.75) | data formatting | bytes 137216 | tf_op jit(solution)/shard_map/cond | solution.py:159
  (3 shorter events, 0.1 us)
Async XLA Ops:
  62.0 5.1 %collective-permute-start = (f32[32,2048]{1,0:T(8,128)S(1)}, f32[32,2048]{1,0:T(8,128)S(1)}, u32[]{:S(2)}, u32[]{:S(2)}) collective-permute-start(f32[32,2048]{1,0:T(8,128)S(1)} %reshape.22), channel_id=1, source_target_pairs={{0,8},{8,0},{1,9},{9,1},{2,10},{10,2},{3,11},{11,3},{4,12},{12,4},... | collective-permute-start | bytes 786440 | tf_op jit(solution)/shard_map/ppermute | solution.py:151

commit v9 on v7

--- a/solution.py
+++ b/solution.py
@@ -47,59 +47,53 @@
         offset += count
 
 
-def normal_kernel(first, count, scale, states_ref, targets_ref, normal_ref, rhs_ref, rows_ref):
-    step = pl.program_id(0)
+def normal_kernel(count, scale, block_ref, states_ref, targets_ref, normal_ref, rhs_ref, rows_ref):
     fill_rows(states_ref, rows_ref)
     feats = rows_ref[...].astype(jnp.bfloat16)
-    chosen = rows_ref[first : first + count, :].astype(jnp.bfloat16)
+    first = block_ref[0] * count
+    window = count + (-count) % 8
+    aligned = pl.multiple_of((first // 8) * 8, 8)
+    lifted = rows_ref[pl.ds(aligned, window), :]
+    shift = (window - (first - aligned)) % window
+    chosen = pltpu.roll(lifted, shift, 0)[0:count, :].astype(jnp.bfloat16)
     dims = (((1,), (1,)), ((), ()))
     normal_part = lax.dot_general(chosen, feats, dims, preferred_element_type=jnp.float32)
     rhs_part = lax.dot_general(chosen, targets_ref[...], dims, preferred_element_type=jnp.float32)
-
-    @pl.when(step == 0)
-    def _():
-        normal_ref[...] = normal_part
-        rhs_ref[...] = rhs_part
-
-    @pl.when(step > 0)
-    def _():
-        normal_ref[...] += normal_part
-        rhs_ref[...] += rhs_part
-
-    @pl.when(step == pl.num_programs(0) - 1)
-    def _():
-        normal_ref[...] = normal_ref[...] / scale
-        rhs_ref[...] = rhs_ref[...] / scale
+    normal_ref[...] = normal_part / scale
+    rhs_ref[...] = rhs_part / scale
 
 
-def normal_block(states, targets, block, blocks, lanes=1024):
+def normal_block(states, targets, block, blocks):
     rank, snaps = states.shape
     width = rank + rank * (rank + 1) // 2
     count = width // blocks
-    kernel = functools.partial(normal_kernel, block * count, count, float(snaps))
+    kernel = functools.partial(normal_kernel, count, float(snaps))
     return pl.pallas_call(
         kernel,
-        grid=(snaps // lanes,),
-        in_specs=[
-            pl.BlockSpec((rank, lanes), lambda j: (0, j)),
-            pl.BlockSpec((rank, lanes), lambda j: (0, j)),
-        ],
-        out_specs=[
-            pl.BlockSpec((count, width), lambda j: (0, 0)),
-            pl.BlockSpec((count, rank), lambda j: (0, 0)),
-        ],
+        grid_spec=pltpu.PrefetchScalarGridSpec(
+            num_scalar_prefetch=1,
+            grid=(1,),
+            in_specs=[
+                pl.BlockSpec((rank, snaps), lambda j, b: (0, 0)),
+                pl.BlockSpec((rank, snaps), lambda j, b: (0, 0)),
+            ],
+            out_specs=[
+                pl.BlockSpec((count, width), lambda j, b: (0, 0)),
+                pl.BlockSpec((count, rank), lambda j, b: (0, 0)),
+            ],
+            scratch_shapes=[pltpu.VMEM((width, snaps), jnp.float32)],
+        ),
         out_shape=[
             jax.ShapeDtypeStruct((count, width), jnp.float32),
             jax.ShapeDtypeStruct((count, rank), jnp.float32),
         ],
-        scratch_shapes=[pltpu.VMEM((width, lanes), jnp.float32)],
         compiler_params=pltpu.CompilerParams(vmem_limit_bytes=48 * 1024 * 1024),
         cost_estimate=pl.CostEstimate(
             flops=2 * count * (width + rank) * snaps,
             transcendentals=0,
             bytes_accessed=rank * snaps * 6 + count * (width + rank) * 4,
         ),
-    )(states, targets)
+    )(jnp.reshape(block, (1,)).astype(jnp.int32), states, targets)
 
 
 def per_device(snapshots, basis):
@@ -123,8 +117,7 @@
         jnp.concatenate([other, half], axis=0),
     )
     targets = (jnp.roll(states, -1, axis=1) - states).astype(jnp.bfloat16)
-    branches = [functools.partial(normal_block, block=b, blocks=snaps) for b in range(snaps)]
-    normal, rhs = lax.switch(lax.axis_index("snap"), branches, states, targets)
+    normal, rhs = normal_block(states, targets, lax.axis_index("snap"), snaps)
     return (normal, rhs)
 
 

time: 68.1 us -> 70.1 us (1.029)
  Pallas kernels: 5.56 us -> 7.58 us
    pallas_call x1, Pallas kernels: 5.56 us -> 7.58 us  [normal_block(): pl.pallas_call(kernel, grid_spec=pltpu.PrefetchScalarGridSpec(num_scalar_...]
    cond x1 -> x0, local copies, waits for them, and re-layouts: 0.76 us -> none  [per_device(): normal, rhs = lax.switch(lax.axis_index('snap'), branches, states, targets)]
    pallas_call x0 -> x1, local copies, waits for them, and re-layouts: none -> 0.76 us  [normal_block(): pl.pallas_call(kernel, grid_spec=pltpu.PrefetchScalarGridSpec(num_scalar_...]
where the time goes in v9:
time: 70.1 us; the launch traced here: 69.8 us
  blocking collectives  51.2 us (73%)
  Pallas kernels  7.58 us (11%)
  starting transfers between devices  4.17 us (6%)
  local copies, waits for them, and re-layouts  2.89 us (4%)
  matrix products  1.51 us (2%)
  waiting for transfers between devices  0.95 us (1%)
  other arithmetic  0.83 us (1%)
    all_to_all x1, blocking collectives, per_device(): lax.all_to_all(spread, ('chip', 'snap'), 0, 0, tiled=True)  26.5 us
    all_to_all x1, blocking collectives, per_device(): received = lax.all_to_all(by_chip, ('chip', 'core'), 0, 0, tiled=True)  24.7 us
    pallas_call x1, Pallas kernels, normal_block(): pl.pallas_call(kernel, grid_spec=pltpu.PrefetchScalarGridSpec(num_scalar_...  7.58 us
    ppermute x1, starting transfers between devices, per_device(): other = lax.ppermute(half, 'core', [(0, 1), (1, 0)])  4.17 us
    unnamed x2, local copies, waits for them, and re-layouts  1.59 us
    dot_general x1, matrix products, per_device(): lax.dot_general(basis, snapshots, (((0,), (0,)), ((), ())), preferred_ele...  1.51 us
  transfers between devices with their start and end apart: 1, of which 1 were waited for; matrix products, arithmetic and copies ran while one was open for 0% of the time, Pallas kernels for 0%

profile of v9, /device:TPU:1, one launch (start us, length us, event | category | flops | bytes accessed | tf_op | source)
XLA Modules:
  0.0 69.8 jit_solution(7088205164235678413)
XLA Ops:
  0.6 0.0 copy-start
  0.6 1.6 %copy-done = bf16[4096,256]{1,0:T(8,128)(2,1)S(1)} copy-done((bf16[4096,256]{1,0:T(8,128)(2,1)S(1)}, bf16[4096,256]{1,0:T(8,128)(2,1)}, u32[]{:S(2)}) %copy-start) | copy-done | bytes 2097176
  2.2 1.5 %fusion.1 = f32[64,256]{1,0:T(8,128)S(1)} fusion(bf16[4096,64]{0,1:T(8,128)(2,1)} %param.3, bf16[4096,256]{1,0:T(8,128)(2,1)S(1)} %copy-done), kind=kOutput, calls=%fused_computation.4 | convolution fusion | flops 134217728 | bytes 2686976 | tf_op jit(solution)/shard_map/dot_general | solution.py:100
  3.7 0.1 copy.11
  3.8 0.1 all_to_all.13
  3.9 24.7 %all_to_all.16 = f32[64,1,256]{2,1,0:T(1,128)S(1)} all-to-all(f32[64,1,256]{2,1,0:T(1,128)S(1)} %all_to_all.13), channel_id=1, replica_groups=mesh['chip'=32,'core'=2,'snap'=8] {'chip','core'}, dimensions={0} | all-to-all | bytes 131072 | tf_op jit(solution)/shard_map/all_to_all | solution.py:109
  28.6 0.1 reduce_sum.9
  28.7 0.1 broadcast_in_dim.2
  28.9 26.5 %all_to_all.17 = f32[256,1,256]{2,1,0:T(1,128)S(1)} all-to-all(f32[256,1,256]{2,1,0:T(1,128)S(1)} %broadcast_in_dim.2), channel_id=1, replica_groups=mesh['chip'=32,'core'=2,'snap'=8] {'chip','snap'}, dimensions={0} | all-to-all | bytes 524288 | tf_op jit(solution)/shard_map/all_to_all | solution.py:112
  55.3 0.6 reduce.1
  56.0 4.2 %collective-permute-start = (f32[32,2048]{1,0:T(8,128)S(1)}, f32[32,2048]{1,0:T(8,128)S(1)}, u32[]{:S(2)}, u32[]{:S(2)}) collective-permute-start(f32[32,2048]{1,0:T(8,128)S(1)} %reshape.26), channel_id=1, source_target_pairs={{0,8},{8,0},{1,9},{9,1},{2,10},{10,2},{3,11},{11,3},{4,12},{12,4},... | collective-permute-start | bytes 786440 | tf_op jit(solution)/shard_map/ppermute | solution.py:113
  60.2 1.0 %collective-permute-done = f32[32,2048]{1,0:T(8,128)S(1)} collective-permute-done((f32[32,2048]{1,0:T(8,128)S(1)}, f32[32,2048]{1,0:T(8,128)S(1)}, u32[]{:S(2)}, u32[]{:S(2)}) %collective-permute-start) | collective-permute-done | bytes 262176 | tf_op jit(solution)/shard_map/ppermute | solution.py:113
  61.2 0.2 slice.10
  61.4 0.1 fusion.targets_ref
  61.5 7.6 %shard_map.41 = (f32[268,2144]{1,0:T(8,128)}, f32[268,64]{1,0:T(8,128)S(1)}) custom-call(s32[1]{0:T(128)} %bitcast.block_ref, f32[64,2048]{1,0:T(8,128)S(1)} %maximum_select_fusion.states_ref, bf16[64,2048]{1,0:T(8,128)(2,1)S(1)} %fusion.targets_ref), custom_call_target="tpu_custom_call" | custom-call | flops 2423783424 | bytes 3153408 | tf_op jit(solution)/shard_map/pallas_call | solution.py:71
  69.0 0.8 %copy.9 = f32[268,64]{0,1:T(8,128)} copy(f32[268,64]{1,0:T(8,128)S(1)} %get-tuple-element.7) | data formatting | bytes 137216 | tf_op jit(solution)/shard_map/pallas_call | solution.py:71
  (3 shorter events, 0.1 us)
Async XLA Ops:
  0.6 1.6 %copy-start = (bf16[4096,256]{1,0:T(8,128)(2,1)S(1)}, bf16[4096,256]{1,0:T(8,128)(2,1)}, u32[]{:S(2)}) copy-start(bf16[4096,256]{1,0:T(8,128)(2,1)} %param.2) | copy-start | bytes 6291460
  56.0 5.1 %collective-permute-start = (f32[32,2048]{1,0:T(8,128)S(1)}, f32[32,2048]{1,0:T(8,128)S(1)}, u32[]{:S(2)}, u32[]{:S(2)}) collective-permute-start(f32[32,2048]{1,0:T(8,128)S(1)} %reshape.26), channel_id=1, source_target_pairs={{0,8},{8,0},{1,9},{9,1},{2,10},{10,2},{3,11},{11,3},{4,12},{12,4},... | collective-permute-start | bytes 786440 | tf_op jit(solution)/shard_map/ppermute | solution.py:113

commit v10 on v8

--- a/solution.py
+++ b/solution.py
@@ -103,9 +103,7 @@
 
 
 def project_kernel(basis_ref, snapshots_ref, out_ref):
-    part = lax.dot_general(
-        basis_ref[...], snapshots_ref[...], (((0,), (0,)), ((), ())), preferred_element_type=jnp.float32
-    )
+    part = jnp.dot(basis_ref[...], snapshots_ref[...], preferred_element_type=jnp.float32)
 
     @pl.when(pl.program_id(0) == 0)
     def _():
@@ -116,14 +114,14 @@
         out_ref[...] += part
 
 
-def project(basis, snapshots, depth=512):
-    rows, rank = basis.shape
+def project(basis_t, snapshots, depth=1024):
+    rank, rows = basis_t.shape
     columns = snapshots.shape[1]
     return pl.pallas_call(
         project_kernel,
         grid=(rows // depth,),
         in_specs=[
-            pl.BlockSpec((depth, rank), lambda k: (k, 0)),
+            pl.BlockSpec((rank, depth), lambda k: (0, k)),
             pl.BlockSpec((depth, columns), lambda k: (k, 0)),
         ],
         out_specs=pl.BlockSpec((rank, columns), lambda k: (0, 0)),
@@ -133,11 +131,11 @@
             transcendentals=0,
             bytes_accessed=rows * (rank + columns) * 2 + rank * columns * 4,
         ),
-    )(basis, snapshots)
+    )(basis_t, snapshots)
 
 
 def per_device(snapshots, basis):
-    partial_value = project(basis, snapshots)
+    partial_value = project(basis.T, snapshots)
     rank, columns = partial_value.shape
     chips = lax.axis_size("chip")
     cores = lax.axis_size("core")

time: 74.1 us -> 69.3 us (0.935)
  local copies, waits for them, and re-layouts: 4.5 us -> 2.14 us
  Pallas kernels: 10.8 us -> 8.45 us
    unnamed x1 -> x0, local copies, waits for them, and re-layouts: 2.36 us -> none
    pallas_call x1, Pallas kernels: 5.88 us -> 3.56 us  [project(): pl.pallas_call(project_kernel, grid=(rows // depth,), in_specs=[pl.BlockS...]
where the time goes in v10:
time: 69.3 us; the launch traced here: 69 us
  blocking collectives  51.2 us (74%)
  Pallas kernels  8.45 us (12%)
  starting transfers between devices  3.99 us (6%)
  local copies, waits for them, and re-layouts  2.14 us (3%)
  waiting for transfers between devices  1.13 us (2%)
  between operations  0.93 us (1%)
  other arithmetic  0.83 us (1%)
    all_to_all x1, blocking collectives, per_device(): lax.all_to_all(spread, ('chip', 'snap'), 0, 0, tiled=True)  26.5 us
    all_to_all x1, blocking collectives, per_device(): received = lax.all_to_all(by_chip, ('chip', 'core'), 0, 0, tiled=True)  24.7 us
    pallas_call x1, Pallas kernels, normal_block(): pl.pallas_call(kernel, grid=(snaps // lanes,), in_specs=[pl.BlockSpec((ra...  4.89 us
    ppermute x1, starting transfers between devices, per_device(): other = lax.ppermute(half, 'core', [(0, 1), (1, 0)])  3.99 us
    pallas_call x1, Pallas kernels, project(): pl.pallas_call(project_kernel, grid=(rows // depth,), in_specs=[pl.BlockS...  3.56 us
  transfers between devices with their start and end apart: 1, of which 1 were waited for; matrix products, arithmetic and copies ran while one was open for 0% of the time, Pallas kernels for 0%

profile of v10, /device:TPU:1, one launch (start us, length us, event | category | flops | bytes accessed | tf_op | source)
XLA Modules:
  0.0 69.0 jit_solution(17073203648703210097)
XLA Ops:
  0.6 3.6 %shard_map.57 = f32[64,256]{1,0:T(8,128)} custom-call(bf16[64,4096]{1,0:T(8,128)(2,1)} %bitcast.5, bf16[4096,256]{1,0:T(8,128)(2,1)} %snapshots_ref.1), custom_call_target="tpu_custom_call" | custom-call | flops 134217728 | bytes 2686976 | tf_op jit(solution)/shard_map/pallas_call | solution.py:120
  4.2 0.9 %copy.35 = f32[2,32,256]{2,0,1:T(2,128)S(1)} copy(f32[2,32,256]{2,1,0:T(8,128)} %bitcast.7) | data formatting | bytes 131072 | tf_op jit(solution)/shard_map/reshape | solution.py:144
  5.1 0.1 all_to_all.13
  5.2 24.7 %all_to_all.16 = f32[64,1,256]{2,1,0:T(1,128)S(1)} all-to-all(f32[64,1,256]{2,1,0:T(1,128)S(1)} %all_to_all.13), channel_id=1, replica_groups=mesh['chip'=32,'core'=2,'snap'=8] {'chip','core'}, dimensions={0} | all-to-all | bytes 131072 | tf_op jit(solution)/shard_map/all_to_all | solution.py:145
  29.9 0.1 reduce_sum.9
  30.0 0.1 broadcast_in_dim.2
  30.1 26.5 %all_to_all.17 = f32[256,1,256]{2,1,0:T(1,128)S(1)} all-to-all(f32[256,1,256]{2,1,0:T(1,128)S(1)} %broadcast_in_dim.2), channel_id=1, replica_groups=mesh['chip'=32,'core'=2,'snap'=8] {'chip','snap'}, dimensions={0} | all-to-all | bytes 524288 | tf_op jit(solution)/shard_map/all_to_all | solution.py:148
  56.6 0.6 reduce.1
  57.3 4.0 %collective-permute-start = (f32[32,2048]{1,0:T(8,128)S(1)}, f32[32,2048]{1,0:T(8,128)S(1)}, u32[]{:S(2)}, u32[]{:S(2)}) collective-permute-start(f32[32,2048]{1,0:T(8,128)S(1)} %reshape.22), channel_id=1, source_target_pairs={{0,8},{8,0},{1,9},{9,1},{2,10},{10,2},{3,11},{11,3},{4,12},{12,4},... | collective-permute-start | bytes 786440 | tf_op jit(solution)/shard_map/ppermute | solution.py:149
  61.3 1.1 %collective-permute-done = f32[32,2048]{1,0:T(8,128)S(1)} collective-permute-done((f32[32,2048]{1,0:T(8,128)S(1)}, f32[32,2048]{1,0:T(8,128)S(1)}, u32[]{:S(2)}, u32[]{:S(2)}) %collective-permute-start) | collective-permute-done | bytes 262176 | tf_op jit(solution)/shard_map/ppermute | solution.py:149
  62.5 0.2 slice.10
  62.7 0.1 fusion
  62.8 6.0 %conditional.1 = (f32[268,2144]{1,0:T(8,128)}, f32[268,64]{0,1:T(8,128)}) conditional(s32[]{:T(128)} %clamp.3, (f32[64,2048]{1,0:T(8,128)S(1)}, bf16[64,2048]{1,0:T(8,128)(2,1)S(1)}) %tuple.31, (f32[64,2048]{1,0:T(8,128)S(1)}, bf16[64,2048]{1,0:T(8,128)(2,1)S(1)}) %tuple.31, (f32[64,2048]{1,0:T(8,128)S(1)}, ...), branch_computations={%region_1.2_spmd, %region_2.3_spmd, %region_3.4_spmd, %region_4.5_... | conditional | flops 2423783424 | bytes 3290640 | solution.py:157
  62.8 4.9 %branch_0_fun.1 = (f32[268,2144]{1,0:T(8,128)}, f32[268,64]{1,0:T(8,128)S(1)}) custom-call(f32[64,2048]{1,0:T(8,128)S(1)} %get-tuple-element.32.states_ref, bf16[64,2048]{1,0:T(8,128)(2,1)S(1)} %get-tuple-element.33.targets_ref), custom_call_target="tpu_custom_call" | custom-call | flops 2423783424 | bytes 3153408 | tf_op jit(solution)/shard_map/cond/branch_0_fun/pallas_call | solution.py:80
  67.7 0.8 %copy.26 = f32[268,64]{0,1:T(8,128)} copy(f32[268,64]{1,0:T(8,128)S(1)} %get-tuple-element.75) | data formatting | bytes 137216 | tf_op jit(solution)/shard_map/cond | solution.py:157
  (3 shorter events, 0.1 us)
Async XLA Ops:
  57.3 5.1 %collective-permute-start = (f32[32,2048]{1,0:T(8,128)S(1)}, f32[32,2048]{1,0:T(8,128)S(1)}, u32[]{:S(2)}, u32[]{:S(2)}) collective-permute-start(f32[32,2048]{1,0:T(8,128)S(1)} %reshape.22), channel_id=1, source_target_pairs={{0,8},{8,0},{1,9},{9,1},{2,10},{10,2},{3,11},{11,3},{4,12},{12,4},... | collective-permute-start | bytes 786440 | tf_op jit(solution)/shard_map/ppermute | solution.py:149

commit v11 on v7

--- a/solution.py
+++ b/solution.py
@@ -54,7 +54,7 @@
     chosen = rows_ref[first : first + count, :].astype(jnp.bfloat16)
     dims = (((1,), (1,)), ((), ()))
     normal_part = lax.dot_general(chosen, feats, dims, preferred_element_type=jnp.float32)
-    rhs_part = lax.dot_general(chosen, targets_ref[...], dims, preferred_element_type=jnp.float32)
+    rhs_part = lax.dot_general(targets_ref[...], chosen, dims, preferred_element_type=jnp.float32)
 
     @pl.when(step == 0)
     def _():
@@ -72,7 +72,7 @@
         rhs_ref[...] = rhs_ref[...] / scale
 
 
-def normal_block(states, targets, block, blocks, lanes=1024):
+def normal_block(states, targets, block, blocks, lanes=2048):
     rank, snaps = states.shape
     width = rank + rank * (rank + 1) // 2
     count = width // blocks
@@ -86,11 +86,11 @@
         ],
         out_specs=[
             pl.BlockSpec((count, width), lambda j: (0, 0)),
-            pl.BlockSpec((count, rank), lambda j: (0, 0)),
+            pl.BlockSpec((rank, count), lambda j: (0, 0)),
         ],
         out_shape=[
             jax.ShapeDtypeStruct((count, width), jnp.float32),
-            jax.ShapeDtypeStruct((count, rank), jnp.float32),
+            jax.ShapeDtypeStruct((rank, count), jnp.float32),
         ],
         scratch_shapes=[pltpu.VMEM((width, lanes), jnp.float32)],
         compiler_params=pltpu.CompilerParams(vmem_limit_bytes=48 * 1024 * 1024),
@@ -124,8 +124,8 @@
     )
     targets = (jnp.roll(states, -1, axis=1) - states).astype(jnp.bfloat16)
     branches = [functools.partial(normal_block, block=b, blocks=snaps) for b in range(snaps)]
-    normal, rhs = lax.switch(lax.axis_index("snap"), branches, states, targets)
-    return (normal, rhs)
+    normal, rhs_t = lax.switch(lax.axis_index("snap"), branches, states, targets)
+    return (normal, rhs_t.T)
 
 
 def solution(mesh):

time: 68.1 us -> 66.5 us (0.977)
  Pallas kernels: 5.56 us -> 4.74 us
  local copies, waits for them, and re-layouts: 2.89 us -> 2.13 us
    pallas_call x1, Pallas kernels: 5.56 us -> 4.74 us  [normal_block(): pl.pallas_call(kernel, grid=(snaps // lanes,), in_specs=[pl.BlockSpec((ra...]
    cond x1 -> x0, local copies, waits for them, and re-layouts: 0.76 us -> none  [per_device(): normal, rhs = lax.switch(lax.axis_index('snap'), branches, states, targets)]
where the time goes in v11:
time: 66.5 us; the launch traced here: 66.2 us
  blocking collectives  51.2 us (77%)
  Pallas kernels  4.74 us (7%)
  starting transfers between devices  3.99 us (6%)
  local copies, waits for them, and re-layouts  2.13 us (3%)
  matrix products  1.51 us (2%)
  waiting for transfers between devices  1.13 us (2%)
  other arithmetic  0.83 us (1%)
  between operations  0.7 us (1%)
    all_to_all x1, blocking collectives, per_device(): lax.all_to_all(spread, ('chip', 'snap'), 0, 0, tiled=True)  26.5 us
    all_to_all x1, blocking collectives, per_device(): received = lax.all_to_all(by_chip, ('chip', 'core'), 0, 0, tiled=True)  24.7 us
    pallas_call x1, Pallas kernels, normal_block(): pl.pallas_call(kernel, grid=(snaps // lanes,), in_specs=[pl.BlockSpec((ra...  4.74 us
    ppermute x1, starting transfers between devices, per_device(): other = lax.ppermute(half, 'core', [(0, 1), (1, 0)])  3.99 us
    unnamed x2, local copies, waits for them, and re-layouts  1.59 us
    dot_general x1, matrix products, per_device(): lax.dot_general(basis, snapshots, (((0,), (0,)), ((), ())), preferred_ele...  1.51 us
  transfers between devices with their start and end apart: 1, of which 1 were waited for; matrix products, arithmetic and copies ran while one was open for 0% of the time, Pallas kernels for 0%

profile of v11, /device:TPU:1, one launch (start us, length us, event | category | flops | bytes accessed | tf_op | source)
XLA Modules:
  0.0 66.2 jit_solution(595835275786333748)
XLA Ops:
  0.6 0.0 copy-start
  0.6 1.6 %copy-done = bf16[4096,256]{1,0:T(8,128)(2,1)S(1)} copy-done((bf16[4096,256]{1,0:T(8,128)(2,1)S(1)}, bf16[4096,256]{1,0:T(8,128)(2,1)}, u32[]{:S(2)}) %copy-start) | copy-done | bytes 2097176
  2.2 1.5 %fusion.1 = f32[64,256]{1,0:T(8,128)S(1)} fusion(bf16[4096,64]{0,1:T(8,128)(2,1)} %param.11, bf16[4096,256]{1,0:T(8,128)(2,1)S(1)} %copy-done), kind=kOutput, calls=%fused_computation.4 | convolution fusion | flops 134217728 | bytes 2686976 | tf_op jit(solution)/shard_map/dot_general | solution.py:106
  3.7 0.1 copy.8
  3.8 0.1 all_to_all.13
  3.9 24.7 %all_to_all.16 = f32[64,1,256]{2,1,0:T(1,128)S(1)} all-to-all(f32[64,1,256]{2,1,0:T(1,128)S(1)} %all_to_all.13), channel_id=1, replica_groups=mesh['chip'=32,'core'=2,'snap'=8] {'chip','core'}, dimensions={0} | all-to-all | bytes 131072 | tf_op jit(solution)/shard_map/all_to_all | solution.py:115
  28.6 0.1 reduce_sum.9
  28.7 0.1 broadcast_in_dim.2
  28.9 26.5 %all_to_all.17 = f32[256,1,256]{2,1,0:T(1,128)S(1)} all-to-all(f32[256,1,256]{2,1,0:T(1,128)S(1)} %broadcast_in_dim.2), channel_id=1, replica_groups=mesh['chip'=32,'core'=2,'snap'=8] {'chip','snap'}, dimensions={0} | all-to-all | bytes 524288 | tf_op jit(solution)/shard_map/all_to_all | solution.py:118
  55.3 0.6 reduce.1
  56.0 4.0 %collective-permute-start = (f32[32,2048]{1,0:T(8,128)S(1)}, f32[32,2048]{1,0:T(8,128)S(1)}, u32[]{:S(2)}, u32[]{:S(2)}) collective-permute-start(f32[32,2048]{1,0:T(8,128)S(1)} %reshape.22), channel_id=1, source_target_pairs={{0,8},{8,0},{1,9},{9,1},{2,10},{10,2},{3,11},{11,3},{4,12},{12,4},... | collective-permute-start | bytes 786440 | tf_op jit(solution)/shard_map/ppermute | solution.py:119
  60.0 1.1 %collective-permute-done = f32[32,2048]{1,0:T(8,128)S(1)} collective-permute-done((f32[32,2048]{1,0:T(8,128)S(1)}, f32[32,2048]{1,0:T(8,128)S(1)}, u32[]{:S(2)}, u32[]{:S(2)}) %collective-permute-start) | collective-permute-done | bytes 262176 | tf_op jit(solution)/shard_map/ppermute | solution.py:119
  61.2 0.2 slice.10
  61.4 0.1 fusion
  61.5 4.8 %conditional.1 = ((f32[268,2144]{1,0:T(8,128)}, f32[64,268]{1,0:T(8,128)})) conditional(s32[]{:T(128)} %clamp.3, (f32[64,2048]{1,0:T(8,128)S(1)}, bf16[64,2048]{1,0:T(8,128)(2,1)S(1)}) %tuple.32, (f32[64,2048]{1,0:T(8,128)S(1)}, bf16[64,2048]{1,0:T(8,128)(2,1)S(1)}) %tuple.32, (f32[64,2048]{1,0:T(8,128)S(1)}, ...), branch_computations={%region_1.2_spmd, %region_2.3_spmd, %region_3.4_spmd, %region_4.5_... | conditional | flops 2423783424 | bytes 3153416 | solution.py:127
  61.5 4.7 %branch_0_fun.1 = (f32[268,2144]{1,0:T(8,128)}, f32[64,268]{1,0:T(8,128)}) custom-call(f32[64,2048]{1,0:T(8,128)S(1)} %get-tuple-element.32.states_ref, bf16[64,2048]{1,0:T(8,128)(2,1)S(1)} %get-tuple-element.33.targets_ref), custom_call_target="tpu_custom_call" | custom-call | flops 2423783424 | bytes 3153408 | tf_op jit(solution)/shard_map/cond/branch_0_fun/pallas_call | solution.py:80
  (3 shorter events, 0.1 us)
Async XLA Ops:
  0.6 1.6 %copy-start = (bf16[4096,256]{1,0:T(8,128)(2,1)S(1)}, bf16[4096,256]{1,0:T(8,128)(2,1)}, u32[]{:S(2)}) copy-start(bf16[4096,256]{1,0:T(8,128)(2,1)} %param.10) | copy-start | bytes 6291460
  56.0 5.1 %collective-permute-start = (f32[32,2048]{1,0:T(8,128)S(1)}, f32[32,2048]{1,0:T(8,128)S(1)}, u32[]{:S(2)}, u32[]{:S(2)}) collective-permute-start(f32[32,2048]{1,0:T(8,128)S(1)} %reshape.22), channel_id=1, source_target_pairs={{0,8},{8,0},{1,9},{9,1},{2,10},{10,2},{3,11},{11,3},{4,12},{12,4},... | collective-permute-start | bytes 786440 | tf_op jit(solution)/shard_map/ppermute | solution.py:119

commit v12 on v11

--- a/solution.py
+++ b/solution.py
@@ -110,18 +110,13 @@
     chips = lax.axis_size("chip")
     cores = lax.axis_size("core")
     snaps = lax.axis_size("snap")
-    core = lax.axis_index("core")
-    by_chip = partial_value.reshape(cores, chips, columns).transpose(1, 0, 2).reshape(rank, columns)
-    received = lax.all_to_all(by_chip, ("chip", "core"), 0, 0, tiled=True)
+    pair = partial_value.reshape(cores, chips, columns).transpose(1, 0, 2)
+    send = jnp.broadcast_to(pair[:, None], (chips, cores, cores, columns)).reshape(rank, cores, columns)
+    received = lax.all_to_all(send, ("chip", "core"), 0, 0, tiled=True)
     owned = jnp.sum(received, axis=0, keepdims=True)
-    spread = jnp.broadcast_to(owned, (chips * snaps, columns))
-    half = lax.all_to_all(spread, ("chip", "snap"), 0, 0, tiled=True).reshape(chips, snaps * columns)
-    other = lax.ppermute(half, "core", [(0, 1), (1, 0)])
-    states = jnp.where(
-        core == 0,
-        jnp.concatenate([half, other], axis=0),
-        jnp.concatenate([other, half], axis=0),
-    )
+    spread = jnp.broadcast_to(owned, (chips * snaps, cores, columns))
+    rows = lax.all_to_all(spread, ("chip", "snap"), 0, 0, tiled=True)
+    states = rows.reshape(chips, snaps, cores, columns).transpose(2, 0, 1, 3).reshape(rank, snaps * columns)
     targets = (jnp.roll(states, -1, axis=1) - states).astype(jnp.bfloat16)
     branches = [functools.partial(normal_block, block=b, blocks=snaps) for b in range(snaps)]
     normal, rhs_t = lax.switch(lax.axis_index("snap"), branches, states, targets)

time: 66.5 us -> 68.6 us (1.032)
  blocking collectives: 51.2 us -> 25.7 us
  waiting for transfers between devices: 1.13 us -> 19.7 us
  starting transfers between devices: 3.99 us -> 12.6 us
  local copies, waits for them, and re-layouts: 2.13 us -> 3.01 us
    all_to_all x2 -> x1, blocking collectives: 51.2 us -> 25.7 us  [per_device(): received = lax.all_to_all(send, ('chip', 'core'), 0, 0, tiled=True)]
    all_to_all x0 -> x1, waiting for transfers between devices: none -> 19.7 us  [per_device(): rows = lax.all_to_all(spread, ('chip', 'snap'), 0, 0, tiled=True)]
    all_to_all x0 -> x1, starting transfers between devices: none -> 12.6 us  [per_device(): rows = lax.all_to_all(spread, ('chip', 'snap'), 0, 0, tiled=True)]
    ppermute x1 -> x0, starting transfers between devices: 3.99 us -> none  [per_device(): other = lax.ppermute(half, 'core', [(0, 1), (1, 0)])]
    ppermute x1 -> x0, waiting for transfers between devices: 1.13 us -> none  [per_device(): other = lax.ppermute(half, 'core', [(0, 1), (1, 0)])]
    broadcast_in_dim x1 -> x2, local copies, waits for them, and re-layouts: 0.14 us -> 0.97 us  [the longest x1 0.93 us: per_device(): spread = jnp.broadcast_to(owned, (chips * snaps, cores, columns))]
    unnamed x2 -> x3, local copies, waits for them, and re-layouts: 1.59 us -> 1.75 us
where the time goes in v12:
time: 68.6 us; the launch traced here: 68.1 us
  blocking collectives  25.7 us (37%)
  waiting for transfers between devices  19.7 us (29%)
  starting transfers between devices  12.6 us (18%)
  Pallas kernels  4.74 us (7%)
  local copies, waits for them, and re-layouts  3.01 us (4%)
  matrix products  1.51 us (2%)
  between operations  0.69 us (1%)
    all_to_all x1, blocking collectives, per_device(): received = lax.all_to_all(send, ('chip', 'core'), 0, 0, tiled=True)  25.7 us
    all_to_all x1, waiting for transfers between devices, per_device(): rows = lax.all_to_all(spread, ('chip', 'snap'), 0, 0, tiled=True)  19.7 us
    all_to_all x1, starting transfers between devices, per_device(): rows = lax.all_to_all(spread, ('chip', 'snap'), 0, 0, tiled=True)  12.6 us
    pallas_call x1, Pallas kernels, normal_block(): pl.pallas_call(kernel, grid=(snaps // lanes,), in_specs=[pl.BlockSpec((ra...  4.74 us
    unnamed x3, local copies, waits for them, and re-layouts  1.75 us
    dot_general x1, matrix products, per_device(): lax.dot_general(basis, snapshots, (((0,), (0,)), ((), ())), preferred_ele...  1.51 us
  transfers between devices with their start and end apart: 1, of which 1 were waited for; matrix products, arithmetic and copies ran while one was open for 0% of the time, Pallas kernels for 0%

profile of v12, /device:TPU:1, one launch (start us, length us, event | category | flops | bytes accessed | tf_op | source)
XLA Modules:
  0.0 68.1 jit_solution(2332081305853741971)
XLA Ops:
  0.6 0.0 copy-start
  0.6 1.6 %copy-done = bf16[4096,256]{1,0:T(8,128)(2,1)S(1)} copy-done((bf16[4096,256]{1,0:T(8,128)(2,1)S(1)}, bf16[4096,256]{1,0:T(8,128)(2,1)}, u32[]{:S(2)}) %copy-start) | copy-done | bytes 2097176
  2.2 1.5 %fusion.1 = f32[64,256]{1,0:T(8,128)S(1)} fusion(bf16[4096,64]{0,1:T(8,128)(2,1)} %param.11, bf16[4096,256]{1,0:T(8,128)(2,1)S(1)} %copy-done), kind=kOutput, calls=%fused_computation.2 | convolution fusion | flops 134217728 | bytes 2686976 | tf_op jit(solution)/shard_map/dot_general | solution.py:106
  3.7 0.1 copy.8
  3.8 25.7 %all_to_all.10 = f32[64,2,256]{2,1,0:T(2,128)S(1)} all-to-all(f32[64,2,256]{2,1,0:T(2,128)S(1)} %bitcast.26), channel_id=1, replica_groups=mesh['chip'=32,'core'=2,'snap'=8] {'chip','core'}, dimensions={0} | all-to-all | bytes 262144 | tf_op jit(solution)/shard_map/all_to_all | solution.py:115
  29.6 0.1 reduce_sum.9
  29.6 0.9 %broadcast_in_dim.5 = f32[256,2,256]{2,1,0:T(2,128)} broadcast(f32[2,256]{1,0:T(2,128)S(1)} %reduce_sum.9), dimensions={1,2} | broadcast | bytes 526336 | tf_op jit(solution)/shard_map/broadcast_in_dim | solution.py:117
  30.6 12.6 %all-to-all-start.1 = ((f32[256,2,256]{2,1,0:T(2,128)}), f32[256,2,256]{2,1,0:T(2,128)S(1)}, u32[]{:S(2)}, u32[]{:S(2)}) async-start(f32[256,2,256]{2,1,0:T(2,128)} %broadcast_in_dim.5), calls=%async_computation.1 | async-start | bytes 1048576 | tf_op jit(solution)/shard_map/all_to_all | solution.py:118
  43.1 19.7 %all-to-all-done.1 = f32[256,2,256]{2,1,0:T(2,128)S(1)} async-done(((f32[256,2,256]{2,1,0:T(2,128)}), f32[256,2,256]{2,1,0:T(2,128)S(1)}, u32[]{:S(2)}, u32[]{:S(2)}) %all-to-all-start.1) | async-done | bytes 524320 | tf_op jit(solution)/shard_map/all_to_all | solution.py:118
  62.9 0.2 copy.12
  63.0 0.2 slice.10
  63.2 0.1 fusion
  63.3 4.8 %conditional.1 = ((f32[268,2144]{1,0:T(8,128)}, f32[64,268]{1,0:T(8,128)})) conditional(s32[]{:T(128)} %clamp.3, (f32[64,2048]{1,0:T(8,128)S(1)}, bf16[64,2048]{1,0:T(8,128)(2,1)S(1)}) %tuple.50, (f32[64,2048]{1,0:T(8,128)S(1)}, bf16[64,2048]{1,0:T(8,128)(2,1)S(1)}) %tuple.51, (f32[64,2048]{1,0:T(8,128)S(1)}, ...), branch_computations={%region_1.2_spmd, %region_2.3_spmd, %region_3.4_spmd, %region_4.5_... | conditional | flops 2423783424 | bytes 3153416 | solution.py:122
  63.3 4.7 %branch_0_fun.1 = (f32[268,2144]{1,0:T(8,128)}, f32[64,268]{1,0:T(8,128)}) custom-call(f32[64,2048]{1,0:T(8,128)S(1)} %get-tuple-element.32.states_ref, bf16[64,2048]{1,0:T(8,128)(2,1)S(1)} %get-tuple-element.33.targets_ref), custom_call_target="tpu_custom_call" | custom-call | flops 2423783424 | bytes 3153408 | tf_op jit(solution)/shard_map/cond/branch_0_fun/pallas_call | solution.py:80
  (3 shorter events, 0.1 us)
Async XLA Ops:
  0.6 1.6 %copy-start = (bf16[4096,256]{1,0:T(8,128)(2,1)S(1)}, bf16[4096,256]{1,0:T(8,128)(2,1)}, u32[]{:S(2)}) copy-start(bf16[4096,256]{1,0:T(8,128)(2,1)} %param.10) | copy-start | bytes 6291460
  30.6 32.2 %all-to-all-start.1 = ((f32[256,2,256]{2,1,0:T(2,128)}), f32[256,2,256]{2,1,0:T(2,128)S(1)}, u32[]{:S(2)}, u32[]{:S(2)}) async-start(f32[256,2,256]{2,1,0:T(2,128)} %broadcast_in_dim.5), calls=%async_computation.1 | async-start | bytes 1048576 | tf_op jit(solution)/shard_map/all_to_all | solution.py:118

commit v13 on v11

--- a/solution.py
+++ b/solution.py
@@ -47,14 +47,17 @@
         offset += count
 
 
-def normal_kernel(first, count, scale, states_ref, targets_ref, normal_ref, rhs_ref, rows_ref):
+def normal_kernel(first, count, scale, states_ref, normal_ref, rhs_ref, rows_ref):
     step = pl.program_id(0)
     fill_rows(states_ref, rows_ref)
     feats = rows_ref[...].astype(jnp.bfloat16)
     chosen = rows_ref[first : first + count, :].astype(jnp.bfloat16)
     dims = (((1,), (1,)), ((), ()))
     normal_part = lax.dot_general(chosen, feats, dims, preferred_element_type=jnp.float32)
-    rhs_part = lax.dot_general(targets_ref[...], chosen, dims, preferred_element_type=jnp.float32)
+    snaps = states_ref.shape[1]
+    following = pltpu.roll(states_ref[...], snaps - 1, 1)
+    targets = (following - states_ref[...]).astype(jnp.bfloat16)
+    rhs_part = lax.dot_general(targets, chosen, dims, preferred_element_type=jnp.float32)
 
     @pl.when(step == 0)
     def _():
@@ -72,7 +75,7 @@
         rhs_ref[...] = rhs_ref[...] / scale
 
 
-def normal_block(states, targets, block, blocks, lanes=2048):
+def normal_block(states, block, blocks, lanes=2048):
     rank, snaps = states.shape
     width = rank + rank * (rank + 1) // 2
     count = width // blocks
@@ -80,10 +83,7 @@
     return pl.pallas_call(
         kernel,
         grid=(snaps // lanes,),
-        in_specs=[
-            pl.BlockSpec((rank, lanes), lambda j: (0, j)),
-            pl.BlockSpec((rank, lanes), lambda j: (0, j)),
-        ],
+        in_specs=[pl.BlockSpec((rank, lanes), lambda j: (0, j))],
         out_specs=[
             pl.BlockSpec((count, width), lambda j: (0, 0)),
             pl.BlockSpec((rank, count), lambda j: (0, 0)),
@@ -99,7 +99,7 @@
             transcendentals=0,
             bytes_accessed=rank * snaps * 6 + count * (width + rank) * 4,
         ),
-    )(states, targets)
+    )(states)
 
 
 def per_device(snapshots, basis):
@@ -122,9 +122,8 @@
         jnp.concatenate([half, other], axis=0),
         jnp.concatenate([other, half], axis=0),
     )
-    targets = (jnp.roll(states, -1, axis=1) - states).astype(jnp.bfloat16)
     branches = [functools.partial(normal_block, block=b, blocks=snaps) for b in range(snaps)]
-    normal, rhs_t = lax.switch(lax.axis_index("snap"), branches, states, targets)
+    normal, rhs_t = lax.switch(lax.axis_index("snap"), branches, states)
     return (normal, rhs_t.T)
 
 

time: 66.5 us -> 66.2 us (level)
  no operation moved by 1% of the time
where the time goes in v13:
time: 66.2 us; the launch traced here: 65.9 us
  blocking collectives  51.2 us (77%)
  Pallas kernels  4.75 us (7%)
  starting transfers between devices  3.99 us (6%)
  local copies, waits for them, and re-layouts  1.93 us (3%)
  matrix products  1.51 us (2%)
  waiting for transfers between devices  1.13 us (2%)
  other arithmetic  0.75 us (1%)
  between operations  0.69 us (1%)
    all_to_all x1, blocking collectives, per_device(): lax.all_to_all(spread, ('chip', 'snap'), 0, 0, tiled=True)  26.5 us
    all_to_all x1, blocking collectives, per_device(): received = lax.all_to_all(by_chip, ('chip', 'core'), 0, 0, tiled=True)  24.7 us
    pallas_call x1, Pallas kernels, normal_block(): pl.pallas_call(kernel, grid=(snaps // lanes,), in_specs=[pl.BlockSpec((ra...  4.75 us
    ppermute x1, starting transfers between devices, per_device(): other = lax.ppermute(half, 'core', [(0, 1), (1, 0)])  3.99 us
    unnamed x2, local copies, waits for them, and re-layouts  1.59 us
    dot_general x1, matrix products, per_device(): lax.dot_general(basis, snapshots, (((0,), (0,)), ((), ())), preferred_ele...  1.51 us
  transfers between devices with their start and end apart: 1, of which 1 were waited for; matrix products, arithmetic and copies ran while one was open for 0% of the time, Pallas kernels for 0%

profile of v13, /device:TPU:1, one launch (start us, length us, event | category | flops | bytes accessed | tf_op | source)
XLA Modules:
  0.0 65.9 jit_solution(7052748307399886041)
XLA Ops:
  0.6 0.0 copy-start
  0.6 1.6 %copy-done = bf16[4096,256]{1,0:T(8,128)(2,1)S(1)} copy-done((bf16[4096,256]{1,0:T(8,128)(2,1)S(1)}, bf16[4096,256]{1,0:T(8,128)(2,1)}, u32[]{:S(2)}) %copy-start) | copy-done | bytes 2097176
  2.2 1.5 %fusion = f32[64,256]{1,0:T(8,128)S(1)} fusion(bf16[4096,64]{0,1:T(8,128)(2,1)} %param.11, bf16[4096,256]{1,0:T(8,128)(2,1)S(1)} %copy-done), kind=kOutput, calls=%fused_computation.2 | convolution fusion | flops 134217728 | bytes 2686976 | tf_op jit(solution)/shard_map/dot_general | solution.py:106
  3.7 0.1 copy.8
  3.8 0.1 all_to_all.13
  3.9 24.7 %all_to_all.16 = f32[64,1,256]{2,1,0:T(1,128)S(1)} all-to-all(f32[64,1,256]{2,1,0:T(1,128)S(1)} %all_to_all.13), channel_id=1, replica_groups=mesh['chip'=32,'core'=2,'snap'=8] {'chip','core'}, dimensions={0} | all-to-all | bytes 131072 | tf_op jit(solution)/shard_map/all_to_all | solution.py:115
  28.6 0.1 reduce_sum.9
  28.7 0.1 broadcast_in_dim.2
  28.9 26.5 %all_to_all.17 = f32[256,1,256]{2,1,0:T(1,128)S(1)} all-to-all(f32[256,1,256]{2,1,0:T(1,128)S(1)} %broadcast_in_dim.2), channel_id=1, replica_groups=mesh['chip'=32,'core'=2,'snap'=8] {'chip','snap'}, dimensions={0} | all-to-all | bytes 524288 | tf_op jit(solution)/shard_map/all_to_all | solution.py:118
  55.3 0.6 reduce.1
  56.0 4.0 %collective-permute-start = (f32[32,2048]{1,0:T(8,128)S(1)}, f32[32,2048]{1,0:T(8,128)S(1)}, u32[]{:S(2)}, u32[]{:S(2)}) collective-permute-start(f32[32,2048]{1,0:T(8,128)S(1)} %reshape.22), channel_id=1, source_target_pairs={{0,8},{8,0},{1,9},{9,1},{2,10},{10,2},{3,11},{11,3},{4,12},{12,4},... | collective-permute-start | bytes 786440 | tf_op jit(solution)/shard_map/ppermute | solution.py:119
  60.0 1.1 %collective-permute-done = f32[32,2048]{1,0:T(8,128)S(1)} collective-permute-done((f32[32,2048]{1,0:T(8,128)S(1)}, f32[32,2048]{1,0:T(8,128)S(1)}, u32[]{:S(2)}, u32[]{:S(2)}) %collective-permute-start) | collective-permute-done | bytes 262176 | tf_op jit(solution)/shard_map/ppermute | solution.py:119
  61.2 4.8 %conditional.1 = ((f32[268,2144]{1,0:T(8,128)}, f32[64,268]{1,0:T(8,128)})) conditional(s32[]{:T(128)} %clamp.3, f32[64,2048]{1,0:T(8,128)S(1)} %maximum_select_fusion, f32[64,2048]{1,0:T(8,128)S(1)} %maximum_select_fusion, f32[64,2048]{1,0:T(8,128)S(1)} %maximum_select_fusion, ...), branch_computations={%region_1.2_spmd, %region_2.3_spmd, %region_3.4_spmd, %region_4.5_... | conditional | flops 2423783424 | bytes 3153416 | solution.py:126
  61.2 4.7 %branch_0_fun.1 = (f32[268,2144]{1,0:T(8,128)}, f32[64,268]{1,0:T(8,128)}) custom-call(f32[64,2048]{1,0:T(8,128)S(1)} %states_ref), custom_call_target="tpu_custom_call" | custom-call | flops 2423783424 | bytes 3153408 | tf_op jit(solution)/shard_map/cond/branch_0_fun/pallas_call | solution.py:83
  (2 shorter events, 0.1 us)
Async XLA Ops:
  0.6 1.6 %copy-start = (bf16[4096,256]{1,0:T(8,128)(2,1)S(1)}, bf16[4096,256]{1,0:T(8,128)(2,1)}, u32[]{:S(2)}) copy-start(bf16[4096,256]{1,0:T(8,128)(2,1)} %param.10) | copy-start | bytes 6291460
  56.0 5.1 %collective-permute-start = (f32[32,2048]{1,0:T(8,128)S(1)}, f32[32,2048]{1,0:T(8,128)S(1)}, u32[]{:S(2)}, u32[]{:S(2)}) collective-permute-start(f32[32,2048]{1,0:T(8,128)S(1)} %reshape.22), channel_id=1, source_target_pairs={{0,8},{8,0},{1,9},{9,1},{2,10},{10,2},{3,11},{11,3},{4,12},{12,4},... | collective-permute-start | bytes 786440 | tf_op jit(solution)/shard_map/ppermute | solution.py:119
